TPU v7x, 32 devices: a whole 2x2x4 slice. The times are simulated.
32 devices in a mesh: grp: 2 (over y), srv: 16 (over z, x, core).
Axes of the slice: x: 2, y: 2, z: 4, core: 2. Of those that a mesh axis runs over, the one named last changes fastest.
Arguments:
- queries: bfloat16 [12288, 1536], P(('grp', 'srv')), parts along dimension 0, may hold values from -4096 to 4096
- latent_rope: bfloat16 [12288, 576], P(('grp', 'srv')), parts along dimension 0, may hold values from -16 to 16
- doc_start: int32 [12288], P(('grp', 'srv')), parts along dimension 0, may hold values from 0 to 6143, as said below
- w_kv_up: bfloat16 [512, 2048], replicated, may hold values from -0.25 to 0.25
- w_out: bfloat16 [1024, 2048], replicated, may hold values from -0.5 to 0.5
Outputs:
- mixed: bfloat16 [12288, 2048], P(('grp', 'srv')), parts along dimension 0
There are 2 independent parts, one for each index of `grp`. A program takes and returns all parts, laid end to end along the dimension named above; an argument that names none is the same for every part. Nothing has to cross between parts.
Inputs may be any that keep to these rules, and one draw needn't show every extreme that they name: doc_start[i] <= i < doc_start[i] + 2688; doc_start[i] is i or doc_start[i-1]; the first document has exactly 2688 positions.
All inputs are finite; a program needn't handle non-finite values.
Results may differ from a plain program's by a relative error of at most 0.0063.
Values may be sent and summed in bfloat16 or wider, within the bound.
No kernel may reach another device: no remote copies, remote signals or barrier semaphores. Data moves between devices by JAX's collectives and lax.ppermute only.
A program may use at most 128 MiB of HBM per device.

v0:
```python
import functools
import math

import jax
import jax.numpy as jnp
from jax import lax
from jax.experimental import pallas as pl
from jax.experimental.pallas import tpu as pltpu
from jax.sharding import PartitionSpec as P

DN = 128
DR = 64
DV = 128
R = 512
REACH = 7


def moved(value, pairs):
    return lax.ppermute(value, "srv", pairs)


def even_distance_blocks(own):
    count = lax.axis_size("srv")
    slots = range(count)
    k_of = lambda s: s % 4
    near = moved(own, [(s, s + 2) for s in slots if k_of(s) < 2])
    back4 = moved(own, [(s, s + 4) for s in slots if s + 4 < count])
    across = moved(back4, [(s, s ^ 2) for s in slots])
    back8 = moved(back4, [(s, s + 4) for s in slots if s + 4 < count and k_of(s) != 0])
    far = moved(back8, [(s, s - 2) for s in slots if k_of(s) >= 2])
    low_half = lax.axis_index("srv") % 4 < 2
    dist2 = jnp.where(low_half, across, near)
    dist6 = jnp.where(low_half, far, across)
    return [own, dist2, back4, dist6, back8]


def odd_distance_block(nearer, farther):
    count = lax.axis_size("srv")
    upper_core = lax.axis_index("srv") % 2 == 1
    sent = jnp.where(upper_core, farther, nearer)
    return moved(sent, [(s, s ^ 1) for s in range(count)])


def distance_kernel(flag_ref, qn_ref, qr_ref, lat_ref, w_ref, rel_ref, o_ref, m_ref, l_ref, *, distance):
    rows = lat_ref.shape[0]

    @pl.when(flag_ref[0] == 0)
    def _():
        o_ref[...] = jnp.zeros(o_ref.shape, jnp.float32)
        m_ref[...] = jnp.full(m_ref.shape, -1e30, jnp.float32)
        l_ref[...] = jnp.zeros(l_ref.shape, jnp.float32)

    @pl.when(flag_ref[0] != 0)
    def _():
        score_scale = 1.0 / math.sqrt(DN + DR)
        kv = jnp.dot(lat_ref[:, :R], w_ref[...], preferred_element_type=jnp.float32).astype(jnp.bfloat16)
        key_nope = kv[:, :DN]
        values = kv[:, DN:]
        key_rope = lat_ref[:, R:]
        contract = (((1,), (1,)), ((), ()))
        scores = lax.dot_general(qn_ref[0], key_nope, contract, preferred_element_type=jnp.float32)
        scores = scores + lax.dot_general(qr_ref[0], key_rope, contract, preferred_element_type=jnp.float32)
        scores = scores * score_scale
        col = lax.broadcasted_iota(jnp.int32, (rows, rows), 1)
        allowed = col >= rel_ref[...] + distance * rows
        if distance == 0:
            allowed = allowed & (col <= lax.broadcasted_iota(jnp.int32, (rows, rows), 0))
        masked = jnp.where(allowed, scores, -jnp.inf)
        block_max = jnp.maximum(jnp.max(masked, axis=1, keepdims=True), jnp.float32(-1e30))
        weights = jnp.where(allowed, jnp.exp(scores - block_max), jnp.float32(0.0))
        l_ref[0] = jnp.sum(weights, axis=1, keepdims=True)
        m_ref[0] = block_max
        o_ref[...] = jnp.dot(weights.astype(jnp.bfloat16), values, preferred_element_type=jnp.float32)


def distance_terms(flag, query_nope, query_rope, latent_block, w_kv_up, rel_start, distance):
    head_count, rows, _ = query_nope.shape
    width = latent_block.shape[1]
    flops = head_count * rows * (2 * R * (DN + DV) + 2 * rows * (DN + DR + DV))
    return pl.pallas_call(
        functools.partial(distance_kernel, distance=distance),
        out_shape=(
            jax.ShapeDtypeStruct((rows, head_count * DV), jnp.float32),
            jax.ShapeDtypeStruct((head_count, rows, 1), jnp.float32),
            jax.ShapeDtypeStruct((head_count, rows, 1), jnp.float32),
        ),
        grid_spec=pltpu.PrefetchScalarGridSpec(
            num_scalar_prefetch=1,
            grid=(head_count,),
            in_specs=[
                pl.BlockSpec((1, rows, DN), lambda h, f: (h, 0, 0)),
                pl.BlockSpec((1, rows, DR), lambda h, f: (h, 0, 0)),
                pl.BlockSpec((rows, width), lambda h, f: (0, 0)),
                pl.BlockSpec((R, DN + DV), lambda h, f: (0, h)),
                pl.BlockSpec((rows, 1), lambda h, f: (0, 0)),
            ],
            out_specs=[
                pl.BlockSpec((rows, DV), lambda h, f: (0, h)),
                pl.BlockSpec((1, rows, 1), lambda h, f: (h, 0, 0)),
                pl.BlockSpec((1, rows, 1), lambda h, f: (h, 0, 0)),
            ],
        ),
        compiler_params=pltpu.CompilerParams(dimension_semantics=("arbitrary",)),
        cost_estimate=pl.CostEstimate(
            flops=flops, transcendentals=head_count * rows * rows, bytes_accessed=6 * 1024 * 1024
        ),
    )(flag, query_nope, query_rope, latent_block, w_kv_up, rel_start)


def merge_blocks(pieces):
    top_max = pieces[0][1]
    for block_part in pieces[1:]:
        top_max = jnp.maximum(top_max, block_part[1])
    numerator = jnp.zeros(pieces[0][0].shape, jnp.float32)
    denominator = jnp.zeros(pieces[0][0].shape[:2] + (1,), jnp.float32)
    for block_part in pieces:
        factor = jnp.exp(block_part[1] - top_max)
        numerator = numerator + factor.T[:, :, None] * block_part[0]
        denominator = denominator + (factor * block_part[2]).T[:, :, None]
    return (numerator / denominator).astype(jnp.bfloat16)


def local(queries, latent_rope, doc_start, w_kv_up, w_out):
    row_count = queries.shape[0]
    head_count = w_out.shape[0] // DV
    query_all = queries.reshape(row_count, head_count, DN + DR).transpose(1, 0, 2)
    query_nope = query_all[:, :, :DN]
    query_rope = query_all[:, :, DN:]
    device_slot = lax.axis_index("srv")
    block_first = device_slot * row_count
    rel_start = (doc_start - block_first).reshape(row_count, 1)
    lowest_start = jnp.min(doc_start)
    evens = even_distance_blocks(latent_rope)
    held_at = {2 * j: evens[j] for j in range(5)}
    for j in range(1, 5):
        held_at[2 * j - 1] = odd_distance_block(evens[j - 1], evens[j])
    pieces = []
    for distance in range(REACH + 1):
        key_last = block_first - distance * row_count + row_count - 1
        flag = (key_last >= lowest_start).astype(jnp.int32).reshape(1)
        block_out, block_max, block_total = distance_terms(
            flag, query_nope, query_rope, held_at[distance], w_kv_up, rel_start, distance
        )
        pieces.append((block_out.reshape(row_count, head_count, DV), block_max[:, :, 0], block_total[:, :, 0]))
    attended = merge_blocks(pieces).reshape(row_count, head_count * DV)
    return jnp.dot(attended, w_out, preferred_element_type=jnp.float32).astype(jnp.bfloat16)


def solution(mesh):
    in_specs = (P(("grp", "srv"), None), P(("grp", "srv"), None), P(("grp", "srv")), P(), P())
    out_specs = P(("grp", "srv"), None)
    return jax.shard_map(local, mesh=mesh, in_specs=in_specs, out_specs=out_specs, check_vma=False)
```

profile of v0, /device:TPU:10, one launch (start us, length us, event | category | flops | bytes accessed | tf_op | source)
XLA Modules:
  0.0 174.8 jit_solution(12088181237748970748)
XLA Ops:
  0.0 2.0 %copy.21.lat_ref = bf16[384,576]{1,0:T(8,128)(2,1)} copy(bf16[384,576]{0,1:T(8,128)(2,1)} %param.6) | data formatting | bytes 884736 | tf_op args[1]
  2.0 3.5 %collective-permute-start = (bf16[384,576]{1,0:T(8,128)(2,1)}, bf16[384,576]{1,0:T(8,128)(2,1)}, u32[]{:S(2)}, u32[]{:S(2)}) collective-permute-start(bf16[384,576]{1,0:T(8,128)(2,1)} %copy.21.lat_ref), channel_id=1, source_target_pairs={{0,4},{1,5},{2,6},{3,7},{4,8},{5,9},{6,10},{7,11},{8,12},{9,13},{1... | collective-permute-start | bytes 1327112 | tf_op jit(solution)/shard_map/ppermute | solution.py:19
  5.5 11.7 %collective-permute-done.lat_ref = bf16[384,576]{1,0:T(8,128)(2,1)} collective-permute-done((bf16[384,576]{1,0:T(8,128)(2,1)}, bf16[384,576]{1,0:T(8,128)(2,1)}, u32[]{:S(2)}, u32[]{:S(2)}) %collective-permute-start) | collective-permute-done | bytes 442400 | tf_op jit(solution)/shard_map/ppermute | solution.py:19
  17.2 3.5 %collective-permute-start.5 = (bf16[384,576]{1,0:T(8,128)(2,1)}, bf16[384,576]{1,0:T(8,128)(2,1)}, u32[]{:S(2)}, u32[]{:S(2)}) collective-permute-start(bf16[384,576]{1,0:T(8,128)(2,1)} %collective-permute-done.lat_ref), channel_id=1, source_target_pairs={{1,5},{2,6},{3,7},{5,9},{6,10},{7,11},{9,13},{10,14},{11,15},{17,2... | collective-permute-start | bytes 1327112 | tf_op jit(solution)/shard_map/ppermute | solution.py:19
  20.7 1.3 collective-permute-start.2
  22.0 3.4 %collective-permute-start.1 = (bf16[384,576]{1,0:T(8,128)(2,1)}, bf16[384,576]{1,0:T(8,128)(2,1)S(1)}, u32[]{:S(2)}, u32[]{:S(2)}) collective-permute-start(bf16[384,576]{1,0:T(8,128)(2,1)} %collective-permute-done.lat_ref), channel_id=1, source_target_pairs={{0,2},{1,3},{2,0},{3,1},{4,6},{5,7},{6,4},{7,5},{8,10},{9,11},{10,... | collective-permute-start | bytes 1327112 | tf_op jit(solution)/shard_map/ppermute | solution.py:19
  25.4 6.1 %collective-permute-done.5 = bf16[384,576]{1,0:T(8,128)(2,1)} collective-permute-done((bf16[384,576]{1,0:T(8,128)(2,1)}, bf16[384,576]{1,0:T(8,128)(2,1)}, u32[]{:S(2)}, u32[]{:S(2)}) %collective-permute-start.5) | collective-permute-done | bytes 442400 | tf_op jit(solution)/shard_map/ppermute | solution.py:19
  31.5 2.1 %collective-permute-start.6 = (bf16[384,576]{1,0:T(8,128)(2,1)}, bf16[384,576]{1,0:T(8,128)(2,1)}, u32[]{:S(2)}, u32[]{:S(2)}) collective-permute-start(bf16[384,576]{1,0:T(8,128)(2,1)} %collective-permute-done.5), channel_id=1, source_target_pairs={{2,0},{3,1},{6,4},{7,5},{10,8},{11,9},{14,12},{15,13},{18,16},{19,... | collective-permute-start | bytes 1327112 | tf_op jit(solution)/shard_map/ppermute | solution.py:19
  33.6 1.3 broadcast_subtract_fusion
  34.9 1.7 copy.19
  36.6 0.7 copy.20
  37.3 1.0 slice.9.qr_ref
  38.3 1.0 slice.8.qn_ref
  44.5 0.8 reshape.114.rel_ref
  45.3 10.5 %shard_map.55 = (f32[384,1024]{1,0:T(8,128)}, f32[8,384,1]{2,1,0:T(8,128)}, f32[8,384,1]{2,1,0:T(8,128)}) custom-call(s32[1]{0:T(128)} %bitcast.flag_ref, bf16[8,384,128]{2,1,0:T(8,128)(2,1)} %slice.8.qn_ref, bf16[8,384,64]{2,1,0:T(8,128)(2,1)} %slice.9.qr_ref, bf16[384,576]{1,0:T(8,128)(2,1)} %copy.21.lat_ref, bf16[512,2048]{1,0:T(8,128)(2,1)} %w_ref.15, ...), custom_call_target="tpu_custom_call" | custom-call | flops 1560281088 | bytes 6291456 | tf_op jit(solution)/shard_map/pallas_call | solution.py:80
  55.8 2.0 %reduce = f32[8,384]{1,0:T(8,128)S(1)} reduce(f32[8,384,1]{2,1,0:T(8,128)} %get-tuple-element.29, f32[]{:T(128)} %constant.81), dimensions={2}, to_apply=%get-tuple-element.29.reduce_sub_computation | reduce | bytes 24580 | tf_op jit(solution)/shard_map/pallas_call | solution.py:80
  57.8 1.1 reduce.8
  58.9 2.1 %broadcast_select_fusion.5 = (bf16[384,576]{1,0:T(8,128)(2,1)}, bf16[384,576]{1,0:T(8,128)(2,1)S(1)}) fusion(bf16[384,576]{1,0:T(8,128)(2,1)} %copy.21.lat_ref, pred[]{:T(512)S(6)} %eq.12, bf16[384,576]{1,0:T(8,128)(2,1)S(1)} %collective-permute-done.1, bf16[384,576]{1,0:T(8,128)(2,1)} %collective-permute-done.2, pred[]{:T(512)S(6)} %lt.21), kind=kLoop, calls=%fused_computation.23 | loop fusion | flops 442368 | bytes 2211842 | tf_op jit(solution)/shard_map/jit(_where)/select_n | solution.py:40
  61.0 1.4 broadcast_select_fusion.3
  62.4 1.0 broadcast_select_fusion.2
  63.3 1.4 collective-permute-start.8
  64.8 10.9 %shard_map.59 = (f32[384,1024]{1,0:T(8,128)}, f32[8,384,1]{2,1,0:T(8,128)}, f32[8,384,1]{2,1,0:T(8,128)}) custom-call(s32[1]{0:T(128)} %bitcast.6.flag_ref, bf16[8,384,128]{2,1,0:T(8,128)(2,1)} %slice.8.qn_ref, bf16[8,384,64]{2,1,0:T(8,128)(2,1)} %slice.9.qr_ref, bf16[384,576]{1,0:T(8,128)(2,1)} %collective-permute-done.lat_ref, bf16[512,2048]{1,0:T(8,128)(2,1)} %w_ref.15, ...), custom_call_target="tpu_custom_call" | custom-call | flops 1560281088 | bytes 6291456 | tf_op jit(solution)/shard_map/pallas_call | solution.py:80
  75.7 2.6 %reduce.4 = f32[8,384]{1,0:T(8,128)} reduce(f32[8,384,1]{2,1,0:T(8,128)} %get-tuple-element.33, f32[]{:T(128)} %constant.81), dimensions={2}, to_apply=%get-tuple-element.33.reduce_sub_computation | reduce | bytes 24580 | tf_op jit(solution)/shard_map/pallas_call | solution.py:80
  78.3 1.1 reduce.12
  79.4 10.9 %shard_map.57 = (f32[384,1024]{1,0:T(8,128)}, f32[8,384,1]{2,1,0:T(8,128)}, f32[8,384,1]{2,1,0:T(8,128)}) custom-call(s32[1]{0:T(128)} %bitcast.4.flag_ref, bf16[8,384,128]{2,1,0:T(8,128)(2,1)} %slice.8.qn_ref, bf16[8,384,64]{2,1,0:T(8,128)(2,1)} %slice.9.qr_ref, bf16[384,576]{1,0:T(8,128)(2,1)} %copy-done.1, bf16[512,2048]{1,0:T(8,128)(2,1)} %w_ref.15, ...), custom_call_target="tpu_custom_call" | custom-call | flops 1560281088 | bytes 6291456 | tf_op jit(solution)/shard_map/pallas_call | solution.py:80
  90.3 2.0 %reduce.2 = f32[8,384]{1,0:T(8,128)S(1)} reduce(f32[8,384,1]{2,1,0:T(8,128)} %get-tuple-element.31, f32[]{:T(128)} %constant.81), dimensions={2}, to_apply=%get-tuple-element.31.reduce_sub_computation | reduce | bytes 24580 | tf_op jit(solution)/shard_map/pallas_call | solution.py:80
  92.3 0.5 reduce.10
  92.8 0.1 collective-permute-start.4
  92.9 10.9 %shard_map.61 = (f32[384,1024]{1,0:T(8,128)}, f32[8,384,1]{2,1,0:T(8,128)}, f32[8,384,1]{2,1,0:T(8,128)}) custom-call(s32[1]{0:T(128)} %bitcast.8.flag_ref, bf16[8,384,128]{2,1,0:T(8,128)(2,1)} %slice.8.qn_ref, bf16[8,384,64]{2,1,0:T(8,128)(2,1)} %slice.9.qr_ref, bf16[384,576]{1,0:T(8,128)(2,1)} %copy-done.2, bf16[512,2048]{1,0:T(8,128)(2,1)} %w_ref.15, ...), custom_call_target="tpu_custom_call" | custom-call | flops 1560281088 | bytes 6291456 | tf_op jit(solution)/shard_map/pallas_call | solution.py:80
  103.8 2.0 %reduce.6 = f32[8,384]{1,0:T(8,128)S(1)} reduce(f32[8,384,1]{2,1,0:T(8,128)} %get-tuple-element.35, f32[]{:T(128)} %constant.81), dimensions={2}, to_apply=%get-tuple-element.35.reduce_sub_computation | reduce | bytes 24580 | tf_op jit(solution)/shard_map/pallas_call | solution.py:80
  105.8 0.5 reduce.14
  106.3 11.0 %shard_map.56 = (f32[384,1024]{1,0:T(8,128)}, f32[8,384,1]{2,1,0:T(8,128)}, f32[8,384,1]{2,1,0:T(8,128)}) custom-call(s32[1]{0:T(128)} %bitcast.3.flag_ref, bf16[8,384,128]{2,1,0:T(8,128)(2,1)} %slice.8.qn_ref, bf16[8,384,64]{2,1,0:T(8,128)(2,1)} %slice.9.qr_ref, bf16[384,576]{1,0:T(8,128)(2,1)} %collective-permute-done.3.lat_ref, bf16[512,2048]{1,0:T(8,128)(2,1)} %w_ref.15, ...), custom_call_target="tpu_custom_call" | custom-call | flops 1560281088 | bytes 6291456 | tf_op jit(solution)/shard_map/pallas_call | solution.py:80
  117.3 2.0 %reduce.1 = f32[8,384]{1,0:T(8,128)S(1)} reduce(f32[8,384,1]{2,1,0:T(8,128)} %get-tuple-element.30, f32[]{:T(128)} %constant.81), dimensions={2}, to_apply=%get-tuple-element.30.reduce_sub_computation | reduce | bytes 24580 | tf_op jit(solution)/shard_map/pallas_call | solution.py:80
  119.3 0.5 reduce.9
  119.8 7.0 %shard_map.62 = (f32[384,1024]{1,0:T(8,128)}, f32[8,384,1]{2,1,0:T(8,128)}, f32[8,384,1]{2,1,0:T(8,128)}) custom-call(s32[1]{0:T(128)} %bitcast.9.flag_ref, bf16[8,384,128]{2,1,0:T(8,128)(2,1)} %slice.8.qn_ref, bf16[8,384,64]{2,1,0:T(8,128)(2,1)} %slice.9.qr_ref, bf16[384,576]{1,0:T(8,128)(2,1)} %collective-permute-done.8.lat_ref, bf16[512,2048]{1,0:T(8,128)(2,1)} %w_ref.15, ...), custom_call_target="tpu_custom_call" | custom-call | flops 1560281088 | bytes 6291456 | tf_op jit(solution)/shard_map/pallas_call | solution.py:80
  126.8 2.0 %reduce.7 = f32[8,384]{1,0:T(8,128)S(1)} reduce(f32[8,384,1]{2,1,0:T(8,128)} %get-tuple-element.36, f32[]{:T(128)} %constant.81), dimensions={2}, to_apply=%get-tuple-element.36.reduce_sub_computation | reduce | bytes 24580 | tf_op jit(solution)/shard_map/pallas_call | solution.py:80
  128.8 0.5 reduce.15
  129.3 11.1 %shard_map.60 = (f32[384,1024]{1,0:T(8,128)}, f32[8,384,1]{2,1,0:T(8,128)}, f32[8,384,1]{2,1,0:T(8,128)}) custom-call(s32[1]{0:T(128)} %bitcast.7.flag_ref, bf16[8,384,128]{2,1,0:T(8,128)(2,1)} %slice.8.qn_ref, bf16[8,384,64]{2,1,0:T(8,128)(2,1)} %slice.9.qr_ref, bf16[384,576]{1,0:T(8,128)(2,1)} %collective-permute-done.7.lat_ref, bf16[512,2048]{1,0:T(8,128)(2,1)} %w_ref.15, ...), custom_call_target="tpu_custom_call" | custom-call | flops 1560281088 | bytes 6291456 | tf_op jit(solution)/shard_map/pallas_call | solution.py:80
  140.4 2.0 %reduce.5 = f32[8,384]{1,0:T(8,128)S(1)} reduce(f32[8,384,1]{2,1,0:T(8,128)} %get-tuple-element.34, f32[]{:T(128)} %constant.81), dimensions={2}, to_apply=%get-tuple-element.34.reduce_sub_computation | reduce | bytes 24580 | tf_op jit(solution)/shard_map/pallas_call | solution.py:80
  142.5 0.5 reduce.13
  143.0 0.8 copy-done.14
  143.7 10.9 %shard_map.58 = (f32[384,1024]{1,0:T(8,128)}, f32[8,384,1]{2,1,0:T(8,128)}, f32[8,384,1]{2,1,0:T(8,128)}) custom-call(s32[1]{0:T(128)} %bitcast.5.flag_ref, bf16[8,384,128]{2,1,0:T(8,128)(2,1)} %slice.8.qn_ref, bf16[8,384,64]{2,1,0:T(8,128)(2,1)} %slice.9.qr_ref, bf16[384,576]{1,0:T(8,128)(2,1)} %copy-done.14, bf16[512,2048]{1,0:T(8,128)(2,1)} %w_ref.15, ...), custom_call_target="tpu_custom_call" | custom-call | flops 1560281088 | bytes 6291456 | tf_op jit(solution)/shard_map/pallas_call | solution.py:80
  154.7 2.0 %reduce.3 = f32[8,384]{1,0:T(8,128)S(1)} reduce(f32[8,384,1]{2,1,0:T(8,128)} %get-tuple-element.32, f32[]{:T(128)} %constant.81), dimensions={2}, to_apply=%get-tuple-element.32.reduce_sub_computation | reduce | bytes 24580 | tf_op jit(solution)/shard_map/pallas_call | solution.py:80
  156.7 0.5 reduce.11
  157.2 0.1 copy.34
  157.4 0.1 copy.33
  157.5 0.1 copy.41
  157.6 0.1 copy.40
  157.8 0.1 copy.39
  157.9 0.1 copy.38
  158.0 0.1 copy.37
  158.2 0.1 copy.36
  158.3 0.1 copy.35
  158.4 0.5 mul.122
  158.9 0.5 mul.125
  159.4 0.5 mul.128
  159.9 0.5 mul.131
  160.3 0.5 mul.134
  160.8 0.5 mul.137
  161.3 0.5 div.11
  161.8 0.5 mul.116
  162.2 0.5 mul.119
  162.7 0.8 copy-done
  163.5 11.3 %convolution_convert_fusion = bf16[384,2048]{1,0:T(8,128)(2,1)} fusion(bf16[1024,2048]{1,0:T(8,128)(2,1)S(1)} %copy-done, f32[48,8,8,128]{3,2,1,0:T(8,128)S(1)} %bitcast.103, f32[384,1024]{1,0:T(8,128)} %get-tuple-element.44, f32[48,8,8,128]{3,2,1,0:T(8,128)S(1)} %bitcast.102, f32[384,1024]{1,0:T(8,128)} %get-tuple-element.43, ...), kind=kOutput, calls=%fused_computation | convolution fusion | flops 1618083840 | bytes 32505856 | tf_op jit(solution)/shard_map/dot_general | solution.py:146
  (39 shorter events, 0.1 us)
Async XLA Ops:
  2.0 15.2 %collective-permute-start = (bf16[384,576]{1,0:T(8,128)(2,1)}, bf16[384,576]{1,0:T(8,128)(2,1)}, u32[]{:S(2)}, u32[]{:S(2)}) collective-permute-start(bf16[384,576]{1,0:T(8,128)(2,1)} %copy.21.lat_ref), channel_id=1, source_target_pairs={{0,4},{1,5},{2,6},{3,7},{4,8},{5,9},{6,10},{7,11},{8,12},{9,13},{1... | collective-permute-start | bytes 1327112 | tf_op jit(solution)/shard_map/ppermute | solution.py:19
  17.2 14.3 %collective-permute-start.5 = (bf16[384,576]{1,0:T(8,128)(2,1)}, bf16[384,576]{1,0:T(8,128)(2,1)}, u32[]{:S(2)}, u32[]{:S(2)}) collective-permute-start(bf16[384,576]{1,0:T(8,128)(2,1)} %collective-permute-done.lat_ref), channel_id=1, source_target_pairs={{1,5},{2,6},{3,7},{5,9},{6,10},{7,11},{9,13},{10,14},{11,15},{17,2... | collective-permute-start | bytes 1327112 | tf_op jit(solution)/shard_map/ppermute | solution.py:19
  20.7 38.2 %collective-permute-start.2 = (bf16[384,576]{1,0:T(8,128)(2,1)}, bf16[384,576]{1,0:T(8,128)(2,1)}, u32[]{:S(2)}, u32[]{:S(2)}) collective-permute-start(bf16[384,576]{1,0:T(8,128)(2,1)} %copy.21.lat_ref), channel_id=1, source_target_pairs={{0,2},{1,3},{4,6},{5,7},{8,10},{9,11},{12,14},{13,15},{16,18},{17,... | collective-permute-start | bytes 1327112 | tf_op jit(solution)/shard_map/ppermute | solution.py:19
  22.0 36.9 %collective-permute-start.1 = (bf16[384,576]{1,0:T(8,128)(2,1)}, bf16[384,576]{1,0:T(8,128)(2,1)S(1)}, u32[]{:S(2)}, u32[]{:S(2)}) collective-permute-start(bf16[384,576]{1,0:T(8,128)(2,1)} %collective-permute-done.lat_ref), channel_id=1, source_target_pairs={{0,2},{1,3},{2,0},{3,1},{4,6},{5,7},{6,4},{7,5},{8,10},{9,11},{10,... | collective-permute-start | bytes 1327112 | tf_op jit(solution)/shard_map/ppermute | solution.py:19
  31.5 29.5 %collective-permute-start.6 = (bf16[384,576]{1,0:T(8,128)(2,1)}, bf16[384,576]{1,0:T(8,128)(2,1)}, u32[]{:S(2)}, u32[]{:S(2)}) collective-permute-start(bf16[384,576]{1,0:T(8,128)(2,1)} %collective-permute-done.5), channel_id=1, source_target_pairs={{2,0},{3,1},{6,4},{7,5},{10,8},{11,9},{14,12},{15,13},{18,16},{19,... | collective-permute-start | bytes 1327112 | tf_op jit(solution)/shard_map/ppermute | solution.py:19
  55.8 2.0 %copy-start.10 = (f32[8,384,1]{2,1,0:T(8,128)S(1)}, f32[8,384,1]{2,1,0:T(8,128)}, u32[]{:S(2)}) copy-start(f32[8,384,1]{2,1,0:T(8,128)} %get-tuple-element.45) | copy-start | bytes 36868
  60.9 1.4 copy-start.1
  60.9 45.4 %collective-permute-start.3 = (bf16[384,576]{1,0:T(8,128)(2,1)}, bf16[384,576]{1,0:T(8,128)(2,1)}, u32[]{:S(2)}, u32[]{:S(2)}) collective-permute-start(bf16[384,576]{1,0:T(8,128)(2,1)} %get-tuple-element.55), channel_id=1, source_target_pairs={{0,1},{1,0},{2,3},{3,2},{4,5},{5,4},{6,7},{7,6},{8,9},{9,8},{10,11... | collective-permute-start | bytes 1327112 | tf_op jit(solution)/shard_map/ppermute | solution.py:19
  62.4 13.3 %copy-start.2 = (bf16[384,576]{1,0:T(8,128)(2,1)}, bf16[384,576]{1,0:T(8,128)(2,1)S(1)}, u32[]{:S(2)}) copy-start(bf16[384,576]{1,0:T(8,128)(2,1)S(1)} %get-tuple-element.58.lat_ref) | copy-start | bytes 1327108
  63.3 56.4 %collective-permute-start.8 = (bf16[384,576]{1,0:T(8,128)(2,1)}, bf16[384,576]{1,0:T(8,128)(2,1)}, u32[]{:S(2)}, u32[]{:S(2)}) collective-permute-start(bf16[384,576]{1,0:T(8,128)(2,1)} %broadcast_select_fusion.2), channel_id=1, source_target_pairs={{0,1},{1,0},{2,3},{3,2},{4,5},{5,4},{6,7},{7,6},{8,9},{9,8},{10,11... | collective-permute-start | bytes 1327112 | tf_op jit(solution)/shard_map/ppermute | solution.py:19
  75.7 2.6 %copy-start.4 = (f32[8,384,1]{2,1,0:T(8,128)S(1)}, f32[8,384,1]{2,1,0:T(8,128)}, u32[]{:S(2)}) copy-start(f32[8,384,1]{2,1,0:T(8,128)} %get-tuple-element.49) | copy-start | bytes 36868
  79.4 49.9 %collective-permute-start.7 = (bf16[384,576]{1,0:T(8,128)(2,1)S(1)}, bf16[384,576]{1,0:T(8,128)(2,1)}, u32[]{:S(2)}, u32[]{:S(2)}) collective-permute-start(bf16[384,576]{1,0:T(8,128)(2,1)S(1)} %get-tuple-element.57), channel_id=1, source_target_pairs={{0,1},{1,0},{2,3},{3,2},{4,5},{5,4},{6,7},{7,6},{8,9},{9,8},{10,11... | collective-permute-start | bytes 1327112 | tf_op jit(solution)/shard_map/ppermute | solution.py:19
  90.3 2.0 %copy-start.5 = (f32[8,384,1]{2,1,0:T(8,128)S(1)}, f32[8,384,1]{2,1,0:T(8,128)}, u32[]{:S(2)}) copy-start(f32[8,384,1]{2,1,0:T(8,128)} %get-tuple-element.47) | copy-start | bytes 36868
  92.8 50.1 %collective-permute-start.4 = (bf16[384,576]{1,0:T(8,128)(2,1)S(1)}, bf16[384,576]{1,0:T(8,128)(2,1)S(1)}, u32[]{:S(2)}, u32[]{:S(2)}) collective-permute-start(bf16[384,576]{1,0:T(8,128)(2,1)S(1)} %get-tuple-element.59), channel_id=1, source_target_pairs={{0,1},{1,0},{2,3},{3,2},{4,5},{5,4},{6,7},{7,6},{8,9},{9,8},{10,11... | collective-permute-start | bytes 1327112 | tf_op jit(solution)/shard_map/ppermute | solution.py:19
  103.8 2.0 %copy-start.6 = (f32[8,384,1]{2,1,0:T(8,128)S(1)}, f32[8,384,1]{2,1,0:T(8,128)}, u32[]{:S(2)}) copy-start(f32[8,384,1]{2,1,0:T(8,128)} %get-tuple-element.51) | copy-start | bytes 36868
  117.3 2.0 %copy-start.7 = (f32[8,384,1]{2,1,0:T(8,128)S(1)}, f32[8,384,1]{2,1,0:T(8,128)}, u32[]{:S(2)}) copy-start(f32[8,384,1]{2,1,0:T(8,128)} %get-tuple-element.46) | copy-start | bytes 36868
  126.8 2.0 %copy-start.8 = (f32[8,384,1]{2,1,0:T(8,128)S(1)}, f32[8,384,1]{2,1,0:T(8,128)}, u32[]{:S(2)}) copy-start(f32[8,384,1]{2,1,0:T(8,128)} %get-tuple-element.52) | copy-start | bytes 36868
  140.4 2.0 %copy-start.9 = (f32[8,384,1]{2,1,0:T(8,128)S(1)}, f32[8,384,1]{2,1,0:T(8,128)}, u32[]{:S(2)}) copy-start(f32[8,384,1]{2,1,0:T(8,128)} %get-tuple-element.50) | copy-start | bytes 36868
  142.9 0.8 copy-start.14
  154.6 2.0 %copy-start.3 = (f32[8,384,1]{2,1,0:T(8,128)S(1)}, f32[8,384,1]{2,1,0:T(8,128)}, u32[]{:S(2)}) copy-start(f32[8,384,1]{2,1,0:T(8,128)} %get-tuple-element.48) | copy-start | bytes 36868
  154.6 2.5 %copy-start.11 = (f32[8,384]{1,0:T(8,128)S(1)}, f32[8,384]{1,0:T(8,128)}, u32[]{:S(2)}) copy-start(f32[8,384]{1,0:T(8,128)} %reduce.4) | copy-start | bytes 36868
  154.6 2.5 %copy-start.12 = (f32[8,384]{1,0:T(8,128)S(1)}, f32[8,384]{1,0:T(8,128)}, u32[]{:S(2)}) copy-start(f32[8,384]{1,0:T(8,128)} %reduce.8) | copy-start | bytes 36868
  154.6 2.5 %copy-start.13 = (f32[8,384]{1,0:T(8,128)S(1)}, f32[8,384]{1,0:T(8,128)}, u32[]{:S(2)}) copy-start(f32[8,384]{1,0:T(8,128)} %reduce.12) | copy-start | bytes 36868
  161.3 2.2 %copy-start = (bf16[1024,2048]{1,0:T(8,128)(2,1)S(1)}, bf16[1024,2048]{1,0:T(8,128)(2,1)}, u32[]{:S(2)}) copy-start(bf16[1024,2048]{1,0:T(8,128)(2,1)} %param.9) | copy-start | bytes 12582916
where the time goes:
time: 177 us; the launch traced here: 175 us
  Pallas kernels  83.3 us (47%)
  other arithmetic  27.4 us (15%)
  waiting for transfers between devices  17.8 us (10%)
  starting transfers between devices  15.2 us (9%)
  local copies, waits for them, and re-layouts  14.2 us (8%)
  matrix products  11.3 us (6%)
  between operations  5.57 us (3%)
    pallas_call x8, Pallas kernels, distance_terms(): pl.pallas_call(functools.partial(distance_kernel, distance=distance), out...  83.3 us
    pallas_call x16, other arithmetic, distance_terms(): pl.pallas_call(functools.partial(distance_kernel, distance=distance), out...  21.6 us
    ppermute x9, waiting for transfers between devices, moved(): return lax.ppermute(value, 'srv', pairs)  17.8 us
    ppermute x9, starting transfers between devices, moved(): return lax.ppermute(value, 'srv', pairs)  15.2 us
    dot_general x1, matrix products, local(): jnp.dot(attended, w_out, preferred_element_type=jnp.float32)  11.3 us
    unnamed x32, local copies, waits for them, and re-layouts  5.31 us
    select_n x3, other arithmetic, odd_distance_block(): sent = jnp.where(upper_core, farther, nearer)  4.43 us
    mul x8, local copies, waits for them, and re-layouts, merge_blocks(): numerator = numerator + factor.T[:, :, None] * block_part[0]  3.76 us
  transfers between devices with their start and end apart: 9, of which 2 were waited for; matrix products, arithmetic and copies ran while one was open for 17% of the time, Pallas kernels for 41%

commit v1 on v0

v1 whole, which is shorter than its diff:
```python
import functools
import math

import jax
import jax.numpy as jnp
from jax import lax
from jax.experimental import pallas as pl
from jax.experimental.pallas import tpu as pltpu
from jax.sharding import PartitionSpec as P

DN = 128
DR = 64
DV = 128
R = 512
REACH = 7


def moved(value, pairs):
    return lax.ppermute(value, "srv", pairs)


def even_distance_blocks(own):
    count = lax.axis_size("srv")
    slots = range(count)
    k_of = lambda s: s % 4
    near = moved(own, [(s, s + 2) for s in slots if k_of(s) < 2])
    back4 = moved(own, [(s, s + 4) for s in slots if s + 4 < count])
    across = moved(back4, [(s, s ^ 2) for s in slots])
    back8 = moved(back4, [(s, s + 4) for s in slots if s + 4 < count and k_of(s) != 0])
    far = moved(back8, [(s, s - 2) for s in slots if k_of(s) >= 2])
    low_half = lax.axis_index("srv") % 4 < 2
    dist2 = jnp.where(low_half, across, near)
    dist6 = jnp.where(low_half, far, across)
    return [own, dist2, back4, dist6, back8]


def odd_distance_block(nearer, farther):
    count = lax.axis_size("srv")
    upper_core = lax.axis_index("srv") % 2 == 1
    sent = jnp.where(upper_core, farther, nearer)
    return moved(sent, [(s, s ^ 1) for s in range(count)])


def attend_kernel(flag_ref, qn_ref, qr_ref, w_ref, rel_ref, *rest):
    latent_refs = rest[: REACH + 1]
    out_ref, o_sc, m_sc, l_sc = rest[REACH + 1 :]
    rows = latent_refs[0].shape[0]
    score_scale = 1.0 / math.sqrt(DN + DR)
    contract = (((1,), (1,)), ((), ()))
    col = lax.broadcasted_iota(jnp.int32, (rows, rows), 1)
    row = lax.broadcasted_iota(jnp.int32, (rows, rows), 0)
    rel = rel_ref[...]
    for distance in range(REACH + 1):
        lat_ref = latent_refs[distance]

        @pl.when(flag_ref[distance] == 0)
        def _():
            o_sc[distance] = jnp.zeros((rows, DV), jnp.float32)
            m_sc[distance] = jnp.full((rows, 1), -1e30, jnp.float32)
            l_sc[distance] = jnp.zeros((rows, 1), jnp.float32)

        @pl.when(flag_ref[distance] != 0)
        def _():
            kv = jnp.dot(lat_ref[:, :R], w_ref[...], preferred_element_type=jnp.float32).astype(jnp.bfloat16)
            scores = lax.dot_general(qn_ref[0], kv[:, :DN], contract, preferred_element_type=jnp.float32)
            scores = scores + lax.dot_general(
                qr_ref[0], lat_ref[:, R:], contract, preferred_element_type=jnp.float32
            )
            scores = scores * score_scale
            allowed = col >= rel + distance * rows
            if distance == 0:
                allowed = allowed & (col <= row)
            masked = jnp.where(allowed, scores, -jnp.inf)
            block_max = jnp.maximum(jnp.max(masked, axis=1, keepdims=True), jnp.float32(-1e30))
            weights = jnp.where(allowed, jnp.exp(scores - block_max), jnp.float32(0.0))
            l_sc[distance] = jnp.sum(weights, axis=1, keepdims=True)
            m_sc[distance] = block_max
            o_sc[distance] = jnp.dot(
                weights.astype(jnp.bfloat16), kv[:, DN:], preferred_element_type=jnp.float32
            )

    top_max = m_sc[0]
    for distance in range(1, REACH + 1):
        top_max = jnp.maximum(top_max, m_sc[distance])
    numerator = jnp.zeros((rows, DV), jnp.float32)
    denominator = jnp.zeros((rows, 1), jnp.float32)
    for distance in range(REACH + 1):
        factor = jnp.exp(m_sc[distance] - top_max)
        numerator = numerator + factor * o_sc[distance]
        denominator = denominator + factor * l_sc[distance]
    out_ref[...] = (numerator / denominator).astype(out_ref.dtype)


def attend(flags, query_nope, query_rope, w_kv_up, rel_start, latent_blocks):
    head_count, rows, _ = query_nope.shape
    width = latent_blocks[0].shape[1]
    blocks = len(latent_blocks)
    flops = head_count * blocks * rows * (2 * R * (DN + DV) + 2 * rows * (DN + DR + DV))
    latent_spec = pl.BlockSpec((rows, width), lambda h, f: (0, 0))
    return pl.pallas_call(
        attend_kernel,
        out_shape=jax.ShapeDtypeStruct((rows, head_count * DV), jnp.bfloat16),
        grid_spec=pltpu.PrefetchScalarGridSpec(
            num_scalar_prefetch=1,
            grid=(head_count,),
            in_specs=[
                pl.BlockSpec((1, rows, DN), lambda h, f: (h, 0, 0)),
                pl.BlockSpec((1, rows, DR), lambda h, f: (h, 0, 0)),
                pl.BlockSpec((R, DN + DV), lambda h, f: (0, h)),
                pl.BlockSpec((rows, 1), lambda h, f: (0, 0)),
            ]
            + [latent_spec] * blocks,
            out_specs=pl.BlockSpec((rows, DV), lambda h, f: (0, h)),
            scratch_shapes=[
                pltpu.VMEM((blocks, rows, DV), jnp.float32),
                pltpu.VMEM((blocks, rows, 1), jnp.float32),
                pltpu.VMEM((blocks, rows, 1), jnp.float32),
            ],
        ),
        compiler_params=pltpu.CompilerParams(dimension_semantics=("arbitrary",)),
        cost_estimate=pl.CostEstimate(
            flops=flops, transcendentals=head_count * blocks * rows * rows, bytes_accessed=8 * 1024 * 1024
        ),
    )(flags, query_nope, query_rope, w_kv_up, rel_start, *latent_blocks)


def local(queries, latent_rope, doc_start, w_kv_up, w_out):
    row_count = queries.shape[0]
    head_count = w_out.shape[0] // DV
    query_all = queries.reshape(row_count, head_count, DN + DR).transpose(1, 0, 2)
    query_nope = query_all[:, :, :DN]
    query_rope = query_all[:, :, DN:]
    device_slot = lax.axis_index("srv")
    block_first = device_slot * row_count
    rel_start = (doc_start - block_first).reshape(row_count, 1)
    lowest_start = jnp.min(doc_start)
    evens = even_distance_blocks(latent_rope)
    held_at = {2 * j: evens[j] for j in range(5)}
    for j in range(1, 5):
        held_at[2 * j - 1] = odd_distance_block(evens[j - 1], evens[j])
    distances = jnp.arange(REACH + 1, dtype=jnp.int32)
    key_last = block_first - distances * row_count + row_count - 1
    flags = (key_last >= lowest_start).astype(jnp.int32)
    attended = attend(
        flags, query_nope, query_rope, w_kv_up, rel_start, [held_at[d] for d in range(REACH + 1)]
    )
    return jnp.dot(attended, w_out, preferred_element_type=jnp.float32).astype(jnp.bfloat16)


def solution(mesh):
    in_specs = (P(("grp", "srv"), None), P(("grp", "srv"), None), P(("grp", "srv")), P(), P())
    out_specs = P(("grp", "srv"), None)
    return jax.shard_map(local, mesh=mesh, in_specs=in_specs, out_specs=out_specs, check_vma=False)
```

time: 177 us -> 124 us (0.70); the launches traced: 175 us -> 124 us
  other arithmetic: 27.4 us -> 4.81 us
  Pallas kernels: 83.3 us -> 63.7 us
  waiting for transfers between devices: 17.8 us -> 32.7 us
  local copies, waits for them, and re-layouts: 14.2 us -> 6.54 us
  matrix products: 11.3 us -> 5.37 us
  between operations: 5.57 us -> 0.14 us
  starting transfers between devices: 15.2 us -> 10.6 us
    pallas_call x16 -> x0, other arithmetic: 21.6 us -> none  [distance_terms(): pl.pallas_call(functools.partial(distance_kernel, distance=distance), out...]
    pallas_call x8 -> x1, Pallas kernels: 83.3 us -> 63.7 us  [attend(): pl.pallas_call(attend_kernel, out_shape=jax.ShapeDtypeStruct((rows, head_...]
    ppermute x9, waiting for transfers between devices: 17.8 us -> 32.7 us  [moved(): return lax.ppermute(value, 'srv', pairs)]
    dot_general x1, matrix products: 11.3 us -> 5.37 us  [local(): jnp.dot(attended, w_out, preferred_element_type=jnp.float32)]
    ppermute x9, starting transfers between devices: 15.2 us -> 10.6 us  [moved(): return lax.ppermute(value, 'srv', pairs)]
    mul x8 -> x0, local copies, waits for them, and re-layouts: 3.76 us -> none  [merge_blocks(): numerator = numerator + factor.T[:, :, None] * block_part[0]]
    unnamed x32 -> x12, local copies, waits for them, and re-layouts: 5.31 us -> 2.98 us
  transfers between devices with their start and end apart: 9 -> 9, of which waited for: 2 -> 4; matrix products, arithmetic and copies ran while one was open for 17% -> 6% of each run, Pallas kernels for 41% -> 0%
where the time goes in v1:
time: 124 us
  Pallas kernels  63.7 us (51%)
  waiting for transfers between devices  32.7 us (26%)
  starting transfers between devices  10.6 us (9%)
  local copies, waits for them, and re-layouts  6.54 us (5%)
  matrix products  5.37 us (4%)
  other arithmetic  4.81 us (4%)
    pallas_call x1, Pallas kernels, attend(): pl.pallas_call(attend_kernel, out_shape=jax.ShapeDtypeStruct((rows, head_...  63.7 us
    ppermute x9, waiting for transfers between devices, moved(): return lax.ppermute(value, 'srv', pairs)  32.7 us
    ppermute x9, starting transfers between devices, moved(): return lax.ppermute(value, 'srv', pairs)  10.6 us
    dot_general x1, matrix products, local(): jnp.dot(attended, w_out, preferred_element_type=jnp.float32)  5.37 us
    unnamed x12, local copies, waits for them, and re-layouts  2.98 us
    select_n x3, other arithmetic, odd_distance_block(): sent = jnp.where(upper_core, farther, nearer)  2.9 us
  transfers between devices with their start and end apart: 9, of which 4 were waited for; matrix products, arithmetic and copies ran while one was open for 6% of the time, Pallas kernels for 0%

profile of v1, /device:TPU:10, one launch (start us, length us, event | category | flops | bytes accessed | tf_op | source)
XLA Modules:
  0.0 123.9 jit_solution(3802743439944988070)
XLA Ops:
  0.0 1.3 %copy.16.rest_0_ = bf16[384,576]{1,0:T(8,128)(2,1)S(1)} copy(bf16[384,576]{0,1:T(8,128)(2,1)} %param.6) | data formatting | bytes 884736 | tf_op args[1]
  1.3 0.0 copy-start.2
  1.3 3.5 %collective-permute-start = (bf16[384,576]{1,0:T(8,128)(2,1)S(1)}, bf16[384,576]{1,0:T(8,128)(2,1)S(1)}, u32[]{:S(2)}, u32[]{:S(2)}) collective-permute-start(bf16[384,576]{1,0:T(8,128)(2,1)S(1)} %copy.16.rest_0_), channel_id=1, source_target_pairs={{0,4},{1,5},{2,6},{3,7},{4,8},{5,9},{6,10},{7,11},{8,12},{9,13},{1... | collective-permute-start | bytes 1327112 | tf_op jit(solution)/shard_map/ppermute | solution.py:19
  4.8 11.4 %collective-permute-done.rest_4_ = bf16[384,576]{1,0:T(8,128)(2,1)S(1)} collective-permute-done((bf16[384,576]{1,0:T(8,128)(2,1)S(1)}, bf16[384,576]{1,0:T(8,128)(2,1)S(1)}, u32[]{:S(2)}, u32[]{:S(2)}) %collective-permute-start) | collective-permute-done | bytes 442400 | tf_op jit(solution)/shard_map/ppermute | solution.py:19
  16.1 0.0 copy-start.3
  16.1 3.5 %collective-permute-start.5 = (bf16[384,576]{1,0:T(8,128)(2,1)S(1)}, bf16[384,576]{1,0:T(8,128)(2,1)S(1)}, u32[]{:S(2)}, u32[]{:S(2)}) collective-permute-start(bf16[384,576]{1,0:T(8,128)(2,1)S(1)} %collective-permute-done.rest_4_), channel_id=1, source_target_pairs={{1,5},{2,6},{3,7},{5,9},{6,10},{7,11},{9,13},{10,14},{11,15},{17,2... | collective-permute-start | bytes 1327112 | tf_op jit(solution)/shard_map/ppermute | solution.py:19
  19.6 0.1 collective-permute-start.1
  19.7 10.4 %collective-permute-done.5 = bf16[384,576]{1,0:T(8,128)(2,1)S(1)} collective-permute-done((bf16[384,576]{1,0:T(8,128)(2,1)S(1)}, bf16[384,576]{1,0:T(8,128)(2,1)S(1)}, u32[]{:S(2)}, u32[]{:S(2)}) %collective-permute-start.5) | collective-permute-done | bytes 442400 | tf_op jit(solution)/shard_map/ppermute | solution.py:19
  30.1 1.3 %collective-permute-start.6 = (bf16[384,576]{1,0:T(8,128)(2,1)S(1)}, bf16[384,576]{1,0:T(8,128)(2,1)S(1)}, u32[]{:S(2)}, u32[]{:S(2)}) collective-permute-start(bf16[384,576]{1,0:T(8,128)(2,1)S(1)} %collective-permute-done.5), channel_id=1, source_target_pairs={{2,0},{3,1},{6,4},{7,5},{10,8},{11,9},{14,12},{15,13},{18,16},{19,... | collective-permute-start | bytes 1327112 | tf_op jit(solution)/shard_map/ppermute | solution.py:19
  31.4 1.3 %collective-permute-start.2 = (bf16[384,576]{1,0:T(8,128)(2,1)S(1)}, bf16[384,576]{1,0:T(8,128)(2,1)S(1)}, u32[]{:S(2)}, u32[]{:S(2)}) collective-permute-start(bf16[384,576]{1,0:T(8,128)(2,1)S(1)} %copy.16.rest_0_), channel_id=1, source_target_pairs={{0,2},{1,3},{4,6},{5,7},{8,10},{9,11},{12,14},{13,15},{16,18},{17,... | collective-permute-start | bytes 1327112 | tf_op jit(solution)/shard_map/ppermute | solution.py:19
  32.8 0.0 collective-permute-done.1
  32.8 7.7 %collective-permute-done.6 = bf16[384,576]{1,0:T(8,128)(2,1)S(1)} collective-permute-done((bf16[384,576]{1,0:T(8,128)(2,1)S(1)}, bf16[384,576]{1,0:T(8,128)(2,1)S(1)}, u32[]{:S(2)}, u32[]{:S(2)}) %collective-permute-start.6) | collective-permute-done | bytes 442400 | tf_op jit(solution)/shard_map/ppermute | solution.py:19
  40.4 0.9 broadcast_select_fusion.2
  41.3 0.0 copy-start
  41.3 3.3 %collective-permute-done.2 = bf16[384,576]{1,0:T(8,128)(2,1)S(1)} collective-permute-done((bf16[384,576]{1,0:T(8,128)(2,1)S(1)}, bf16[384,576]{1,0:T(8,128)(2,1)S(1)}, u32[]{:S(2)}, u32[]{:S(2)}) %collective-permute-start.2) | collective-permute-done | bytes 442400 | tf_op jit(solution)/shard_map/ppermute | solution.py:19
  44.6 1.1 broadcast_select_fusion.4
  45.7 0.0 copy-done.3
  45.7 0.0 copy-start.1
  45.7 0.0 copy-done.2
  45.7 0.9 broadcast_select_fusion.5
  46.6 0.0 copy-done
  46.6 0.0 collective-permute-start.3
  46.6 0.5 collective-permute-start.4
  47.1 0.0 collective-permute-start.7
  47.1 0.5 collective-permute-start.8
  47.6 1.7 %copy.10 = bf16[384,1536]{0,1:T(8,128)(2,1)S(1)} copy(bf16[384,1536]{1,0:T(8,128)(2,1)} %param.5) | data formatting | bytes 2359296 | tf_op args[0]
  49.3 0.0 copy-done.1
  49.4 0.7 copy.11
  50.1 0.0 copy-start.4
  50.1 1.0 slice.8.qn_ref
  51.1 1.0 slice.9.qr_ref
  52.1 0.0 copy-done.4
  52.1 0.7 broadcast_subtract_fusion
  52.8 0.8 reshape.8.rel_ref
  53.7 1.2 compare_convert_fusion.flag_ref
  54.9 0.0 collective-permute-done.3.rest_1_
  54.9 0.0 collective-permute-done.4.rest_3_
  54.9 0.0 collective-permute-done.7.rest_5_
  54.9 0.0 collective-permute-done.8.rest_7_
  54.9 63.7 %shard_map.55 = bf16[384,1024]{1,0:T(8,128)(2,1)} custom-call(s32[8]{0:T(128)} %compare_convert_fusion.flag_ref, bf16[8,384,128]{2,1,0:T(8,128)(2,1)} %slice.8.qn_ref, bf16[8,384,64]{2,1,0:T(8,128)(2,1)} %slice.9.qr_ref, bf16[512,2048]{1,0:T(8,128)(2,1)} %w_ref.1, s32[384,1]{1,0:T(8,128)} %reshape.8.rel_ref, bf16[384,576]{1,0:T(8,128)(2,1)} %copy-done.2, ...), custom_call_target="tpu_custom_call" | custom-call | flops 12482248704 | bytes 8388608 | tf_op jit(solution)/shard_map/pallas_call | solution.py:100
  118.6 5.4 %convolution_convert_fusion = bf16[384,2048]{1,0:T(8,128)(2,1)} fusion(bf16[384,1024]{1,0:T(8,128)(2,1)} %shard_map.55, bf16[1024,2048]{1,0:T(8,128)(2,1)} %param.9), kind=kOutput, calls=%fused_computation | convolution fusion | flops 1611399168 | bytes 6553600 | tf_op jit(solution)/shard_map/dot_general | solution.py:147
Async XLA Ops:
  1.3 44.4 %copy-start.2 = (bf16[384,576]{1,0:T(8,128)(2,1)}, bf16[384,576]{1,0:T(8,128)(2,1)S(1)}, u32[]{:S(2)}) copy-start(bf16[384,576]{1,0:T(8,128)(2,1)S(1)} %copy.16.rest_0_) | copy-start | bytes 1327108
  1.3 14.9 %collective-permute-start = (bf16[384,576]{1,0:T(8,128)(2,1)S(1)}, bf16[384,576]{1,0:T(8,128)(2,1)S(1)}, u32[]{:S(2)}, u32[]{:S(2)}) collective-permute-start(bf16[384,576]{1,0:T(8,128)(2,1)S(1)} %copy.16.rest_0_), channel_id=1, source_target_pairs={{0,4},{1,5},{2,6},{3,7},{4,8},{5,9},{6,10},{7,11},{8,12},{9,13},{1... | collective-permute-start | bytes 1327112 | tf_op jit(solution)/shard_map/ppermute | solution.py:19
  16.1 29.6 %copy-start.3 = (bf16[384,576]{1,0:T(8,128)(2,1)}, bf16[384,576]{1,0:T(8,128)(2,1)S(1)}, u32[]{:S(2)}) copy-start(bf16[384,576]{1,0:T(8,128)(2,1)S(1)} %collective-permute-done.rest_4_) | copy-start | bytes 1327108
  16.1 14.0 %collective-permute-start.5 = (bf16[384,576]{1,0:T(8,128)(2,1)S(1)}, bf16[384,576]{1,0:T(8,128)(2,1)S(1)}, u32[]{:S(2)}, u32[]{:S(2)}) collective-permute-start(bf16[384,576]{1,0:T(8,128)(2,1)S(1)} %collective-permute-done.rest_4_), channel_id=1, source_target_pairs={{1,5},{2,6},{3,7},{5,9},{6,10},{7,11},{9,13},{10,14},{11,15},{17,2... | collective-permute-start | bytes 1327112 | tf_op jit(solution)/shard_map/ppermute | solution.py:19
  19.6 13.2 %collective-permute-start.1 = (bf16[384,576]{1,0:T(8,128)(2,1)S(1)}, bf16[384,576]{1,0:T(8,128)(2,1)S(1)}, u32[]{:S(2)}, u32[]{:S(2)}) collective-permute-start(bf16[384,576]{1,0:T(8,128)(2,1)S(1)} %collective-permute-done.rest_4_), channel_id=1, source_target_pairs={{0,2},{1,3},{2,0},{3,1},{4,6},{5,7},{6,4},{7,5},{8,10},{9,11},{10,... | collective-permute-start | bytes 1327112 | tf_op jit(solution)/shard_map/ppermute | solution.py:19
  30.1 10.3 %collective-permute-start.6 = (bf16[384,576]{1,0:T(8,128)(2,1)S(1)}, bf16[384,576]{1,0:T(8,128)(2,1)S(1)}, u32[]{:S(2)}, u32[]{:S(2)}) collective-permute-start(bf16[384,576]{1,0:T(8,128)(2,1)S(1)} %collective-permute-done.5), channel_id=1, source_target_pairs={{2,0},{3,1},{6,4},{7,5},{10,8},{11,9},{14,12},{15,13},{18,16},{19,... | collective-permute-start | bytes 1327112 | tf_op jit(solution)/shard_map/ppermute | solution.py:19
  31.4 13.1 %collective-permute-start.2 = (bf16[384,576]{1,0:T(8,128)(2,1)S(1)}, bf16[384,576]{1,0:T(8,128)(2,1)S(1)}, u32[]{:S(2)}, u32[]{:S(2)}) collective-permute-start(bf16[384,576]{1,0:T(8,128)(2,1)S(1)} %copy.16.rest_0_), channel_id=1, source_target_pairs={{0,2},{1,3},{4,6},{5,7},{8,10},{9,11},{12,14},{13,15},{16,18},{17,... | collective-permute-start | bytes 1327112 | tf_op jit(solution)/shard_map/ppermute | solution.py:19
  41.3 5.3 %copy-start = (bf16[384,576]{1,0:T(8,128)(2,1)}, bf16[384,576]{1,0:T(8,128)(2,1)S(1)}, u32[]{:S(2)}) copy-start(bf16[384,576]{1,0:T(8,128)(2,1)S(1)} %get-tuple-element.6.rest_6_) | copy-start | bytes 1327108
  45.7 3.7 %copy-start.1 = (bf16[384,576]{1,0:T(8,128)(2,1)}, bf16[384,576]{1,0:T(8,128)(2,1)S(1)}, u32[]{:S(2)}) copy-start(bf16[384,576]{1,0:T(8,128)(2,1)S(1)} %get-tuple-element.8.rest_2_) | copy-start | bytes 1327108
  46.6 8.2 %collective-permute-start.3 = (bf16[384,576]{1,0:T(8,128)(2,1)}, bf16[384,576]{1,0:T(8,128)(2,1)}, u32[]{:S(2)}, u32[]{:S(2)}) collective-permute-start(bf16[384,576]{1,0:T(8,128)(2,1)} %broadcast_select_fusion.5), channel_id=1, source_target_pairs={{0,1},{1,0},{2,3},{3,2},{4,5},{5,4},{6,7},{7,6},{8,9},{9,8},{10,11... | collective-permute-start | bytes 1327112 | tf_op jit(solution)/shard_map/ppermute | solution.py:19
  46.6 8.2 %collective-permute-start.4 = (bf16[384,576]{1,0:T(8,128)(2,1)}, bf16[384,576]{1,0:T(8,128)(2,1)}, u32[]{:S(2)}, u32[]{:S(2)}) collective-permute-start(bf16[384,576]{1,0:T(8,128)(2,1)} %get-tuple-element.7), channel_id=1, source_target_pairs={{0,1},{1,0},{2,3},{3,2},{4,5},{5,4},{6,7},{7,6},{8,9},{9,8},{10,11... | collective-permute-start | bytes 1327112 | tf_op jit(solution)/shard_map/ppermute | solution.py:19
  47.1 7.7 %collective-permute-start.7 = (bf16[384,576]{1,0:T(8,128)(2,1)}, bf16[384,576]{1,0:T(8,128)(2,1)}, u32[]{:S(2)}, u32[]{:S(2)}) collective-permute-start(bf16[384,576]{1,0:T(8,128)(2,1)} %get-tuple-element.9), channel_id=1, source_target_pairs={{0,1},{1,0},{2,3},{3,2},{4,5},{5,4},{6,7},{7,6},{8,9},{9,8},{10,11... | collective-permute-start | bytes 1327112 | tf_op jit(solution)/shard_map/ppermute | solution.py:19
  47.1 7.7 %collective-permute-start.8 = (bf16[384,576]{1,0:T(8,128)(2,1)}, bf16[384,576]{1,0:T(8,128)(2,1)}, u32[]{:S(2)}, u32[]{:S(2)}) collective-permute-start(bf16[384,576]{1,0:T(8,128)(2,1)} %get-tuple-element.5), channel_id=1, source_target_pairs={{0,1},{1,0},{2,3},{3,2},{4,5},{5,4},{6,7},{7,6},{8,9},{9,8},{10,11... | collective-permute-start | bytes 1327112 | tf_op jit(solution)/shard_map/ppermute | solution.py:19
  50.1 2.1 %copy-start.4 = (s32[384]{0:T(512)S(1)}, s32[384]{0:T(512)}, u32[]{:S(2)}) copy-start(s32[384]{0:T(512)} %param.7) | copy-start | bytes 4612

commit v2 on v1

--- a/solution.py
+++ b/solution.py
@@ -41,17 +41,27 @@
     return moved(sent, [(s, s ^ 1) for s in range(count)])
 
 
-def attend_kernel(flag_ref, qn_ref, qr_ref, w_ref, rel_ref, *rest):
+def attend_kernel(flag_ref, qn_ref, qr_ref, rel_ref, *rest):
     latent_refs = rest[: REACH + 1]
-    out_ref, o_sc, m_sc, l_sc = rest[REACH + 1 :]
+    kv_refs = rest[REACH + 1 : 2 * (REACH + 1)]
+    out_ref, o_sc, m_sc, l_sc, bias_sc = rest[2 * (REACH + 1) :]
     rows = latent_refs[0].shape[0]
     score_scale = 1.0 / math.sqrt(DN + DR)
     contract = (((1,), (1,)), ((), ()))
-    col = lax.broadcasted_iota(jnp.int32, (rows, rows), 1)
-    row = lax.broadcasted_iota(jnp.int32, (rows, rows), 0)
-    rel = rel_ref[...]
+
+    @pl.when(pl.program_id(0) == 0)
+    def _():
+        col = lax.broadcasted_iota(jnp.int32, (rows, rows), 1)
+        rel = rel_ref[...]
+        for distance in range(REACH + 1):
+            allowed = col >= rel + distance * rows
+            if distance == 0:
+                allowed = allowed & (col <= lax.broadcasted_iota(jnp.int32, (rows, rows), 0))
+            bias_sc[distance] = jnp.where(allowed, jnp.float32(0.0), -jnp.inf)
+
     for distance in range(REACH + 1):
         lat_ref = latent_refs[distance]
+        kv_ref = kv_refs[distance]
 
         @pl.when(flag_ref[distance] == 0)
         def _():
@@ -61,22 +71,17 @@
 
         @pl.when(flag_ref[distance] != 0)
         def _():
-            kv = jnp.dot(lat_ref[:, :R], w_ref[...], preferred_element_type=jnp.float32).astype(jnp.bfloat16)
-            scores = lax.dot_general(qn_ref[0], kv[:, :DN], contract, preferred_element_type=jnp.float32)
+            scores = lax.dot_general(qn_ref[0], kv_ref[:, :DN], contract, preferred_element_type=jnp.float32)
             scores = scores + lax.dot_general(
                 qr_ref[0], lat_ref[:, R:], contract, preferred_element_type=jnp.float32
             )
-            scores = scores * score_scale
-            allowed = col >= rel + distance * rows
-            if distance == 0:
-                allowed = allowed & (col <= row)
-            masked = jnp.where(allowed, scores, -jnp.inf)
+            masked = scores * score_scale + bias_sc[distance]
             block_max = jnp.maximum(jnp.max(masked, axis=1, keepdims=True), jnp.float32(-1e30))
-            weights = jnp.where(allowed, jnp.exp(scores - block_max), jnp.float32(0.0))
+            weights = jnp.exp(masked - block_max)
             l_sc[distance] = jnp.sum(weights, axis=1, keepdims=True)
             m_sc[distance] = block_max
             o_sc[distance] = jnp.dot(
-                weights.astype(jnp.bfloat16), kv[:, DN:], preferred_element_type=jnp.float32
+                weights.astype(jnp.bfloat16), kv_ref[:, DN:], preferred_element_type=jnp.float32
             )
 
     top_max = m_sc[0]
@@ -91,12 +96,13 @@
     out_ref[...] = (numerator / denominator).astype(out_ref.dtype)
 
 
-def attend(flags, query_nope, query_rope, w_kv_up, rel_start, latent_blocks):
+def attend(flags, query_nope, query_rope, rel_start, latent_blocks, kv_blocks):
     head_count, rows, _ = query_nope.shape
     width = latent_blocks[0].shape[1]
     blocks = len(latent_blocks)
-    flops = head_count * blocks * rows * (2 * R * (DN + DV) + 2 * rows * (DN + DR + DV))
+    flops = head_count * blocks * rows * 2 * rows * (DN + DR + DV)
     latent_spec = pl.BlockSpec((rows, width), lambda h, f: (0, 0))
+    kv_spec = pl.BlockSpec((rows, DN + DV), lambda h, f: (0, h))
     return pl.pallas_call(
         attend_kernel,
         out_shape=jax.ShapeDtypeStruct((rows, head_count * DV), jnp.bfloat16),
@@ -106,22 +112,23 @@
             in_specs=[
                 pl.BlockSpec((1, rows, DN), lambda h, f: (h, 0, 0)),
                 pl.BlockSpec((1, rows, DR), lambda h, f: (h, 0, 0)),
-                pl.BlockSpec((R, DN + DV), lambda h, f: (0, h)),
                 pl.BlockSpec((rows, 1), lambda h, f: (0, 0)),
             ]
-            + [latent_spec] * blocks,
+            + [latent_spec] * blocks
+            + [kv_spec] * blocks,
             out_specs=pl.BlockSpec((rows, DV), lambda h, f: (0, h)),
             scratch_shapes=[
                 pltpu.VMEM((blocks, rows, DV), jnp.float32),
                 pltpu.VMEM((blocks, rows, 1), jnp.float32),
                 pltpu.VMEM((blocks, rows, 1), jnp.float32),
+                pltpu.VMEM((blocks, rows, rows), jnp.float32),
             ],
         ),
         compiler_params=pltpu.CompilerParams(dimension_semantics=("arbitrary",)),
         cost_estimate=pl.CostEstimate(
-            flops=flops, transcendentals=head_count * blocks * rows * rows, bytes_accessed=8 * 1024 * 1024
+            flops=flops, transcendentals=head_count * blocks * rows * rows, bytes_accessed=16 * 1024 * 1024
         ),
-    )(flags, query_nope, query_rope, w_kv_up, rel_start, *latent_blocks)
+    )(flags, query_nope, query_rope, rel_start, *latent_blocks, *kv_blocks)
 
 
 def local(queries, latent_rope, doc_start, w_kv_up, w_out):
@@ -141,9 +148,12 @@
     distances = jnp.arange(REACH + 1, dtype=jnp.int32)
     key_last = block_first - distances * row_count + row_count - 1
     flags = (key_last >= lowest_start).astype(jnp.int32)
-    attended = attend(
-        flags, query_nope, query_rope, w_kv_up, rel_start, [held_at[d] for d in range(REACH + 1)]
-    )
+    latent_blocks = [held_at[d] for d in range(REACH + 1)]
+    kv_blocks = [
+        jnp.dot(block[:, :R], w_kv_up, preferred_element_type=jnp.float32).astype(jnp.bfloat16)
+        for block in latent_blocks
+    ]
+    attended = attend(flags, query_nope, query_rope, rel_start, latent_blocks, kv_blocks)
     return jnp.dot(attended, w_out, preferred_element_type=jnp.float32).astype(jnp.bfloat16)
 
 

time: 124 us -> 121 us (0.976); the launches traced: 124 us -> 119 us
  matrix products: 5.37 us -> 24.8 us
  Pallas kernels: 63.7 us -> 46.5 us
  waiting for transfers between devices: 32.7 us -> 17.4 us
  starting transfers between devices: 10.6 us -> 14.9 us
  local copies, waits for them, and re-layouts: 6.54 us -> 10.3 us
    dot_general x0 -> x8, matrix products: none -> 19.4 us  [local(): jnp.dot(block[:, :R], w_kv_up, preferred_element_type=jnp.float32)]
    pallas_call x1, Pallas kernels: 63.7 us -> 46.5 us  [attend(): pl.pallas_call(attend_kernel, out_shape=jax.ShapeDtypeStruct((rows, head_...]
    ppermute x9, waiting for transfers between devices: 32.7 us -> 17.4 us  [moved(): return lax.ppermute(value, 'srv', pairs)]
    ppermute x9, starting transfers between devices: 10.6 us -> 14.9 us  [moved(): return lax.ppermute(value, 'srv', pairs)]
    unnamed x12 -> x20, local copies, waits for them, and re-layouts: 2.98 us -> 4.65 us
  transfers between devices with their start and end apart: 9 -> 9, of which waited for: 4 -> 3; matrix products, arithmetic and copies ran while one was open for 6% -> 24% of each run, Pallas kernels for 0% -> 0%
where the time goes in v2:
time: 121 us; the launch traced here: 119 us
  Pallas kernels  46.5 us (38%)
  matrix products  24.8 us (20%)
  waiting for transfers between devices  17.4 us (14%)
  starting transfers between devices  14.9 us (12%)
  local copies, waits for them, and re-layouts  10.3 us (9%)
  other arithmetic  5.29 us (4%)
    pallas_call x1, Pallas kernels, attend(): pl.pallas_call(attend_kernel, out_shape=jax.ShapeDtypeStruct((rows, head_...  46.5 us
    dot_general x8, matrix products, local(): jnp.dot(block[:, :R], w_kv_up, preferred_element_type=jnp.float32)  19.4 us
    ppermute x9, waiting for transfers between devices, moved(): return lax.ppermute(value, 'srv', pairs)  17.4 us
    ppermute x9, starting transfers between devices, moved(): return lax.ppermute(value, 'srv', pairs)  14.9 us
    dot_general x1, matrix products, local(): jnp.dot(attended, w_out, preferred_element_type=jnp.float32)  5.37 us
    unnamed x20, local copies, waits for them, and re-layouts  4.65 us
    select_n x3, other arithmetic, odd_distance_block(): sent = jnp.where(upper_core, farther, nearer)  3.59 us
  transfers between devices with their start and end apart: 9, of which 3 were waited for; matrix products, arithmetic and copies ran while one was open for 24% of the time, Pallas kernels for 0%

profile of v2, /device:TPU:10, one launch (start us, length us, event | category | flops | bytes accessed | tf_op | source)
XLA Modules:
  0.0 119.3 jit_solution(11571813014835227345)
XLA Ops:
  0.0 0.0 copy-start
  0.0 2.1 %copy.16.rest_0_ = bf16[384,576]{1,0:T(8,128)(2,1)} copy(bf16[384,576]{0,1:T(8,128)(2,1)} %param.6) | data formatting | bytes 884736 | tf_op args[1]
  2.1 3.5 %collective-permute-start = (bf16[384,576]{1,0:T(8,128)(2,1)}, bf16[384,576]{1,0:T(8,128)(2,1)}, u32[]{:S(2)}, u32[]{:S(2)}) collective-permute-start(bf16[384,576]{1,0:T(8,128)(2,1)} %copy.16.rest_0_), channel_id=1, source_target_pairs={{0,4},{1,5},{2,6},{3,7},{4,8},{5,9},{6,10},{7,11},{8,12},{9,13},{1... | collective-permute-start | bytes 1327112 | tf_op jit(solution)/shard_map/ppermute | solution.py:19
  5.6 11.7 %collective-permute-done.rest_4_ = bf16[384,576]{1,0:T(8,128)(2,1)} collective-permute-done((bf16[384,576]{1,0:T(8,128)(2,1)}, bf16[384,576]{1,0:T(8,128)(2,1)}, u32[]{:S(2)}, u32[]{:S(2)}) %collective-permute-start) | collective-permute-done | bytes 442400 | tf_op jit(solution)/shard_map/ppermute | solution.py:19
  17.3 3.5 %collective-permute-start.5 = (bf16[384,576]{1,0:T(8,128)(2,1)}, bf16[384,576]{1,0:T(8,128)(2,1)}, u32[]{:S(2)}, u32[]{:S(2)}) collective-permute-start(bf16[384,576]{1,0:T(8,128)(2,1)} %collective-permute-done.rest_4_), channel_id=1, source_target_pairs={{1,5},{2,6},{3,7},{5,9},{6,10},{7,11},{9,13},{10,14},{11,15},{17,2... | collective-permute-start | bytes 1327112 | tf_op jit(solution)/shard_map/ppermute | solution.py:19
  20.8 1.3 %collective-permute-start.2 = (bf16[384,576]{1,0:T(8,128)(2,1)}, bf16[384,576]{1,0:T(8,128)(2,1)}, u32[]{:S(2)}, u32[]{:S(2)}) collective-permute-start(bf16[384,576]{1,0:T(8,128)(2,1)} %copy.16.rest_0_), channel_id=1, source_target_pairs={{0,2},{1,3},{4,6},{5,7},{8,10},{9,11},{12,14},{13,15},{16,18},{17,... | collective-permute-start | bytes 1327112 | tf_op jit(solution)/shard_map/ppermute | solution.py:19
  22.1 0.0 copy-done
  22.1 0.0 copy-start.4
  22.1 3.2 %convolution_convert_fusion.8.rest_8_ = bf16[384,2048]{1,0:T(8,128)(2,1)} fusion(bf16[512,2048]{1,0:T(8,128)(2,1)S(1)} %copy-done, bf16[384,576]{0,1:T(8,128)(2,1)} %param.6), kind=kOutput, calls=%fused_computation.8 | convolution fusion | flops 806092800 | bytes 4063232 | tf_op jit(solution)/shard_map/dot_general | solution.py:153
  25.3 3.5 %collective-permute-start.1 = (bf16[384,576]{1,0:T(8,128)(2,1)}, bf16[384,576]{1,0:T(8,128)(2,1)}, u32[]{:S(2)}, u32[]{:S(2)}) collective-permute-start(bf16[384,576]{1,0:T(8,128)(2,1)} %collective-permute-done.rest_4_), channel_id=1, source_target_pairs={{0,2},{1,3},{2,0},{3,1},{4,6},{5,7},{6,4},{7,5},{8,10},{9,11},{10,... | collective-permute-start | bytes 1327112 | tf_op jit(solution)/shard_map/ppermute | solution.py:19
  28.7 2.9 %collective-permute-done.5 = bf16[384,576]{1,0:T(8,128)(2,1)} collective-permute-done((bf16[384,576]{1,0:T(8,128)(2,1)}, bf16[384,576]{1,0:T(8,128)(2,1)}, u32[]{:S(2)}, u32[]{:S(2)}) %collective-permute-start.5) | collective-permute-done | bytes 442400 | tf_op jit(solution)/shard_map/ppermute | solution.py:19
  31.6 2.1 %collective-permute-start.6 = (bf16[384,576]{1,0:T(8,128)(2,1)}, bf16[384,576]{1,0:T(8,128)(2,1)}, u32[]{:S(2)}, u32[]{:S(2)}) collective-permute-start(bf16[384,576]{1,0:T(8,128)(2,1)} %collective-permute-done.5), channel_id=1, source_target_pairs={{2,0},{3,1},{6,4},{7,5},{10,8},{11,9},{14,12},{15,13},{18,16},{19,... | collective-permute-start | bytes 1327112 | tf_op jit(solution)/shard_map/ppermute | solution.py:19
  33.7 0.0 copy-done.4
  33.7 0.6 broadcast_subtract_fusion
  34.3 1.7 %copy.10 = bf16[384,1536]{0,1:T(8,128)(2,1)S(1)} copy(bf16[384,1536]{1,0:T(8,128)(2,1)} %param.5) | data formatting | bytes 2359296 | tf_op args[0]
  36.0 1.6 %copy.11 = bf16[384,8,192]{2,0,1:T(8,128)(2,1)} copy(bf16[384,8,192]{0,2,1:T(8,128)(2,1)S(1)} %bitcast.14) | data formatting | bytes 2359296 | tf_op jit(solution)/shard_map/reshape | solution.py:137
  37.6 0.0 copy-start.1
  37.6 2.2 %slice.41.qr_ref = bf16[8,384,64]{2,1,0:T(8,128)(2,1)} slice(bf16[8,384,192]{2,1,0:T(8,128)(2,1)} %bitcast.12), slice={[0:8], [0:384], [128:192]} | slice | bytes 786432 | tf_op jit(solution)/shard_map/slice | solution.py:139
  39.8 0.0 copy-done.1
  39.8 1.0 slice.40.qn_ref
  40.8 0.8 reshape.8.rel_ref
  41.6 1.1 compare_convert_fusion.flag_ref
  42.7 3.1 %convolution_convert_fusion.4.rest_12_ = bf16[384,2048]{1,0:T(8,128)(2,1)} fusion(bf16[512,2048]{1,0:T(8,128)(2,1)S(1)} %copy-done, bf16[384,576]{1,0:T(8,128)(2,1)} %collective-permute-done.rest_4_), kind=kOutput, calls=%fused_computation.4 | convolution fusion | flops 806092800 | bytes 4063232 | tf_op jit(solution)/shard_map/dot_general | solution.py:153
  45.8 0.0 collective-permute-done.1
  45.8 2.9 %collective-permute-done.6 = bf16[384,576]{1,0:T(8,128)(2,1)} collective-permute-done((bf16[384,576]{1,0:T(8,128)(2,1)}, bf16[384,576]{1,0:T(8,128)(2,1)}, u32[]{:S(2)}, u32[]{:S(2)}) %collective-permute-start.6) | collective-permute-done | bytes 442400 | tf_op jit(solution)/shard_map/ppermute | solution.py:19
  48.7 1.1 broadcast_select_fusion.2
  49.8 0.0 copy-start.2
  49.8 2.2 %convolution_convert_fusion.2.rest_14_ = bf16[384,2048]{1,0:T(8,128)(2,1)} fusion(bf16[512,2048]{1,0:T(8,128)(2,1)S(1)} %copy-done, bf16[384,576]{1,0:T(8,128)(2,1)S(1)} %get-tuple-element.6.rest_6_), kind=kOutput, calls=%fused_computation.2 | convolution fusion | flops 806092800 | bytes 4063232 | tf_op jit(solution)/shard_map/dot_general | solution.py:153
  52.0 0.0 collective-permute-done.2
  52.0 0.0 copy-done.2
  52.0 1.4 %broadcast_select_fusion.4 = (bf16[384,576]{1,0:T(8,128)(2,1)S(1)}, bf16[384,576]{1,0:T(8,128)(2,1)S(1)}, bf16[384,576]{1,0:T(8,128)(2,1)S(1)}) fusion(bf16[384,576]{1,0:T(8,128)(2,1)} %collective-permute-done.rest_4_, pred[]{:T(512)S(6)} %eq.12, bf16[384,576]{1,0:T(8,128)(2,1)} %collective-permute-done.1, bf16[384,576]{1,0:T(8,128)(2,1)} %collective-permute-done.2, ...), kind=kLoop, calls=%fused_computation.13 | loop fusion | flops 663552 | bytes 3096578 | tf_op jit(solution)/shard_map/jit(_where)/select_n | solution.py:40
  53.3 0.0 copy-start.3
  53.4 0.1 collective-permute-start.7
  53.4 0.5 collective-permute-start.8
  53.9 2.2 %convolution_convert_fusion.6.rest_10_ = bf16[384,2048]{1,0:T(8,128)(2,1)} fusion(bf16[512,2048]{1,0:T(8,128)(2,1)S(1)} %copy-done, bf16[384,576]{1,0:T(8,128)(2,1)S(1)} %get-tuple-element.8.rest_2_), kind=kOutput, calls=%fused_computation.6 | convolution fusion | flops 806092800 | bytes 4063232 | tf_op jit(solution)/shard_map/dot_general | solution.py:153
  56.1 0.0 copy-done.3
  56.1 1.1 broadcast_select_fusion.5
  57.3 0.1 collective-permute-start.3
  57.3 0.5 collective-permute-start.4
  57.8 0.0 collective-permute-done.8.rest_7_
  57.8 0.0 copy-start.6
  57.8 2.2 %convolution_convert_fusion.1.rest_15_ = bf16[384,2048]{1,0:T(8,128)(2,1)} fusion(bf16[512,2048]{1,0:T(8,128)(2,1)S(1)} %copy-done, bf16[384,576]{1,0:T(8,128)(2,1)S(1)} %collective-permute-done.8.rest_7_), kind=kOutput, calls=%fused_computation.1 | convolution fusion | flops 806092800 | bytes 4063232 | tf_op jit(solution)/shard_map/dot_general | solution.py:153
  60.0 0.0 copy-done.6
  60.0 0.0 collective-permute-done.7.rest_5_
  60.0 0.0 copy-start.5
  60.0 2.2 %convolution_convert_fusion.3.rest_13_ = bf16[384,2048]{1,0:T(8,128)(2,1)} fusion(bf16[512,2048]{1,0:T(8,128)(2,1)S(1)} %copy-done, bf16[384,576]{1,0:T(8,128)(2,1)S(1)} %collective-permute-done.7.rest_5_), kind=kOutput, calls=%fused_computation.3 | convolution fusion | flops 806092800 | bytes 4063232 | tf_op jit(solution)/shard_map/dot_general | solution.py:153
  62.2 0.0 copy-done.5
  62.2 0.0 collective-permute-done.4.rest_3_
  62.2 0.0 copy-start.8
  62.2 2.2 %convolution_convert_fusion.5.rest_11_ = bf16[384,2048]{1,0:T(8,128)(2,1)} fusion(bf16[512,2048]{1,0:T(8,128)(2,1)S(1)} %copy-done, bf16[384,576]{1,0:T(8,128)(2,1)S(1)} %collective-permute-done.4.rest_3_), kind=kOutput, calls=%fused_computation.5 | convolution fusion | flops 806092800 | bytes 4063232 | tf_op jit(solution)/shard_map/dot_general | solution.py:153
  64.4 0.0 copy-done.8
  64.4 0.0 collective-permute-done.3.rest_1_
  64.4 0.0 copy-start.7
  64.4 0.8 copy-done.7
  65.2 2.2 %convolution_convert_fusion.7.rest_9_ = bf16[384,2048]{1,0:T(8,128)(2,1)} fusion(bf16[512,2048]{1,0:T(8,128)(2,1)S(1)} %copy-done, bf16[384,576]{1,0:T(8,128)(2,1)S(1)} %collective-permute-done.3.rest_1_), kind=kOutput, calls=%fused_computation.7 | convolution fusion | flops 806092800 | bytes 4063232 | tf_op jit(solution)/shard_map/dot_general | solution.py:153
  67.4 46.5 %shard_map.55 = bf16[384,1024]{1,0:T(8,128)(2,1)} custom-call(s32[8]{0:T(128)} %compare_convert_fusion.flag_ref, bf16[8,384,128]{2,1,0:T(8,128)(2,1)} %slice.40.qn_ref, bf16[8,384,64]{2,1,0:T(8,128)(2,1)} %slice.41.qr_ref, s32[384,1]{1,0:T(8,128)} %reshape.8.rel_ref, bf16[384,576]{1,0:T(8,128)(2,1)} %copy.16.rest_0_, bf16[384,576]{1,0:T(8,128)(2,1)} %copy-done.7, ...), custom_call_target="tpu_custom_call" | custom-call | flops 6039797760 | bytes 16777216 | tf_op jit(solution)/shard_map/pallas_call | solution.py:106
  113.9 5.4 %convolution_convert_fusion = bf16[384,2048]{1,0:T(8,128)(2,1)} fusion(bf16[384,1024]{1,0:T(8,128)(2,1)} %shard_map.55, bf16[1024,2048]{1,0:T(8,128)(2,1)} %param.9), kind=kOutput, calls=%fused_computation | convolution fusion | flops 1611399168 | bytes 6553600 | tf_op jit(solution)/shard_map/dot_general | solution.py:157
Async XLA Ops:
  0.0 22.1 %copy-start = (bf16[512,2048]{1,0:T(8,128)(2,1)S(1)}, bf16[512,2048]{1,0:T(8,128)(2,1)}, u32[]{:S(2)}) copy-start(bf16[512,2048]{1,0:T(8,128)(2,1)} %param.8) | copy-start | bytes 6291460
  2.1 15.2 %collective-permute-start = (bf16[384,576]{1,0:T(8,128)(2,1)}, bf16[384,576]{1,0:T(8,128)(2,1)}, u32[]{:S(2)}, u32[]{:S(2)}) collective-permute-start(bf16[384,576]{1,0:T(8,128)(2,1)} %copy.16.rest_0_), channel_id=1, source_target_pairs={{0,4},{1,5},{2,6},{3,7},{4,8},{5,9},{6,10},{7,11},{8,12},{9,13},{1... | collective-permute-start | bytes 1327112 | tf_op jit(solution)/shard_map/ppermute | solution.py:19
  17.3 14.3 %collective-permute-start.5 = (bf16[384,576]{1,0:T(8,128)(2,1)}, bf16[384,576]{1,0:T(8,128)(2,1)}, u32[]{:S(2)}, u32[]{:S(2)}) collective-permute-start(bf16[384,576]{1,0:T(8,128)(2,1)} %collective-permute-done.rest_4_), channel_id=1, source_target_pairs={{1,5},{2,6},{3,7},{5,9},{6,10},{7,11},{9,13},{10,14},{11,15},{17,2... | collective-permute-start | bytes 1327112 | tf_op jit(solution)/shard_map/ppermute | solution.py:19
  20.8 31.2 %collective-permute-start.2 = (bf16[384,576]{1,0:T(8,128)(2,1)}, bf16[384,576]{1,0:T(8,128)(2,1)}, u32[]{:S(2)}, u32[]{:S(2)}) collective-permute-start(bf16[384,576]{1,0:T(8,128)(2,1)} %copy.16.rest_0_), channel_id=1, source_target_pairs={{0,2},{1,3},{4,6},{5,7},{8,10},{9,11},{12,14},{13,15},{16,18},{17,... | collective-permute-start | bytes 1327112 | tf_op jit(solution)/shard_map/ppermute | solution.py:19
  22.1 11.6 %copy-start.4 = (s32[384]{0:T(512)S(1)}, s32[384]{0:T(512)}, u32[]{:S(2)}) copy-start(s32[384]{0:T(512)} %param.7) | copy-start | bytes 4612
  25.3 20.5 %collective-permute-start.1 = (bf16[384,576]{1,0:T(8,128)(2,1)}, bf16[384,576]{1,0:T(8,128)(2,1)}, u32[]{:S(2)}, u32[]{:S(2)}) collective-permute-start(bf16[384,576]{1,0:T(8,128)(2,1)} %collective-permute-done.rest_4_), channel_id=1, source_target_pairs={{0,2},{1,3},{2,0},{3,1},{4,6},{5,7},{6,4},{7,5},{8,10},{9,11},{10,... | collective-permute-start | bytes 1327112 | tf_op jit(solution)/shard_map/ppermute | solution.py:19
  31.6 17.1 %collective-permute-start.6 = (bf16[384,576]{1,0:T(8,128)(2,1)}, bf16[384,576]{1,0:T(8,128)(2,1)}, u32[]{:S(2)}, u32[]{:S(2)}) collective-permute-start(bf16[384,576]{1,0:T(8,128)(2,1)} %collective-permute-done.5), channel_id=1, source_target_pairs={{2,0},{3,1},{6,4},{7,5},{10,8},{11,9},{14,12},{15,13},{18,16},{19,... | collective-permute-start | bytes 1327112 | tf_op jit(solution)/shard_map/ppermute | solution.py:19
  37.6 2.2 %copy-start.1 = (bf16[384,8,192]{2,0,1:T(8,128)(2,1)S(1)}, bf16[384,8,192]{2,0,1:T(8,128)(2,1)}, u32[]{:S(2)}) copy-start(bf16[384,8,192]{2,0,1:T(8,128)(2,1)} %copy.11) | copy-start | bytes 3538948
  49.8 2.2 %copy-start.2 = (bf16[384,576]{1,0:T(8,128)(2,1)}, bf16[384,576]{1,0:T(8,128)(2,1)S(1)}, u32[]{:S(2)}) copy-start(bf16[384,576]{1,0:T(8,128)(2,1)S(1)} %get-tuple-element.6.rest_6_) | copy-start | bytes 1327108
  53.3 2.8 %copy-start.3 = (bf16[384,576]{1,0:T(8,128)(2,1)}, bf16[384,576]{1,0:T(8,128)(2,1)S(1)}, u32[]{:S(2)}) copy-start(bf16[384,576]{1,0:T(8,128)(2,1)S(1)} %get-tuple-element.8.rest_2_) | copy-start | bytes 1327108
  53.4 6.6 %collective-permute-start.7 = (bf16[384,576]{1,0:T(8,128)(2,1)S(1)}, bf16[384,576]{1,0:T(8,128)(2,1)S(1)}, u32[]{:S(2)}, u32[]{:S(2)}) collective-permute-start(bf16[384,576]{1,0:T(8,128)(2,1)S(1)} %get-tuple-element.9), channel_id=1, source_target_pairs={{0,1},{1,0},{2,3},{3,2},{4,5},{5,4},{6,7},{7,6},{8,9},{9,8},{10,11... | collective-permute-start | bytes 1327112 | tf_op jit(solution)/shard_map/ppermute | solution.py:19
  53.4 4.4 %collective-permute-start.8 = (bf16[384,576]{1,0:T(8,128)(2,1)S(1)}, bf16[384,576]{1,0:T(8,128)(2,1)S(1)}, u32[]{:S(2)}, u32[]{:S(2)}) collective-permute-start(bf16[384,576]{1,0:T(8,128)(2,1)S(1)} %get-tuple-element.5), channel_id=1, source_target_pairs={{0,1},{1,0},{2,3},{3,2},{4,5},{5,4},{6,7},{7,6},{8,9},{9,8},{10,11... | collective-permute-start | bytes 1327112 | tf_op jit(solution)/shard_map/ppermute | solution.py:19
  57.3 7.2 %collective-permute-start.3 = (bf16[384,576]{1,0:T(8,128)(2,1)S(1)}, bf16[384,576]{1,0:T(8,128)(2,1)S(1)}, u32[]{:S(2)}, u32[]{:S(2)}) collective-permute-start(bf16[384,576]{1,0:T(8,128)(2,1)S(1)} %broadcast_select_fusion.5), channel_id=1, source_target_pairs={{0,1},{1,0},{2,3},{3,2},{4,5},{5,4},{6,7},{7,6},{8,9},{9,8},{10,11... | collective-permute-start | bytes 1327112 | tf_op jit(solution)/shard_map/ppermute | solution.py:19
  57.3 4.9 %collective-permute-start.4 = (bf16[384,576]{1,0:T(8,128)(2,1)S(1)}, bf16[384,576]{1,0:T(8,128)(2,1)S(1)}, u32[]{:S(2)}, u32[]{:S(2)}) collective-permute-start(bf16[384,576]{1,0:T(8,128)(2,1)S(1)} %get-tuple-element.7), channel_id=1, source_target_pairs={{0,1},{1,0},{2,3},{3,2},{4,5},{5,4},{6,7},{7,6},{8,9},{9,8},{10,11... | collective-permute-start | bytes 1327112 | tf_op jit(solution)/shard_map/ppermute | solution.py:19
  57.8 2.2 %copy-start.6 = (bf16[384,576]{1,0:T(8,128)(2,1)}, bf16[384,576]{1,0:T(8,128)(2,1)S(1)}, u32[]{:S(2)}) copy-start(bf16[384,576]{1,0:T(8,128)(2,1)S(1)} %collective-permute-done.8.rest_7_) | copy-start | bytes 1327108
  60.0 2.2 %copy-start.5 = (bf16[384,576]{1,0:T(8,128)(2,1)}, bf16[384,576]{1,0:T(8,128)(2,1)S(1)}, u32[]{:S(2)}) copy-start(bf16[384,576]{1,0:T(8,128)(2,1)S(1)} %collective-permute-done.7.rest_5_) | copy-start | bytes 1327108
  62.2 2.2 %copy-start.8 = (bf16[384,576]{1,0:T(8,128)(2,1)}, bf16[384,576]{1,0:T(8,128)(2,1)S(1)}, u32[]{:S(2)}) copy-start(bf16[384,576]{1,0:T(8,128)(2,1)S(1)} %collective-permute-done.4.rest_3_) | copy-start | bytes 1327108
  64.4 0.8 copy-start.7

commit v3 on v2

--- a/solution.py
+++ b/solution.py
@@ -42,12 +42,13 @@
 
 
 def attend_kernel(flag_ref, qn_ref, qr_ref, rel_ref, *rest):
-    latent_refs = rest[: REACH + 1]
-    kv_refs = rest[REACH + 1 : 2 * (REACH + 1)]
-    out_ref, o_sc, m_sc, l_sc, bias_sc = rest[2 * (REACH + 1) :]
-    rows = latent_refs[0].shape[0]
+    blocks = REACH + 1
+    rope_refs = rest[:blocks]
+    key_refs = rest[blocks : 2 * blocks]
+    value_refs = rest[2 * blocks : 3 * blocks]
+    out_ref, o_sc, m_sc, l_sc, bias_sc = rest[3 * blocks :]
+    rows = value_refs[0].shape[0]
     score_scale = 1.0 / math.sqrt(DN + DR)
-    contract = (((1,), (1,)), ((), ()))
 
     @pl.when(pl.program_id(0) == 0)
     def _():
@@ -60,8 +61,9 @@
             bias_sc[distance] = jnp.where(allowed, jnp.float32(0.0), -jnp.inf)
 
     for distance in range(REACH + 1):
-        lat_ref = latent_refs[distance]
-        kv_ref = kv_refs[distance]
+        rope_ref = rope_refs[distance]
+        key_ref = key_refs[distance]
+        value_ref = value_refs[distance]
 
         @pl.when(flag_ref[distance] == 0)
         def _():
@@ -71,17 +73,15 @@
 
         @pl.when(flag_ref[distance] != 0)
         def _():
-            scores = lax.dot_general(qn_ref[0], kv_ref[:, :DN], contract, preferred_element_type=jnp.float32)
-            scores = scores + lax.dot_general(
-                qr_ref[0], lat_ref[:, R:], contract, preferred_element_type=jnp.float32
-            )
+            scores = jnp.dot(qn_ref[0], key_ref[...], preferred_element_type=jnp.float32)
+            scores = scores + jnp.dot(qr_ref[0], rope_ref[...], preferred_element_type=jnp.float32)
             masked = scores * score_scale + bias_sc[distance]
             block_max = jnp.maximum(jnp.max(masked, axis=1, keepdims=True), jnp.float32(-1e30))
             weights = jnp.exp(masked - block_max)
             l_sc[distance] = jnp.sum(weights, axis=1, keepdims=True)
             m_sc[distance] = block_max
             o_sc[distance] = jnp.dot(
-                weights.astype(jnp.bfloat16), kv_ref[:, DN:], preferred_element_type=jnp.float32
+                weights.astype(jnp.bfloat16), value_ref[...], preferred_element_type=jnp.float32
             )
 
     top_max = m_sc[0]
@@ -96,13 +96,13 @@
     out_ref[...] = (numerator / denominator).astype(out_ref.dtype)
 
 
-def attend(flags, query_nope, query_rope, rel_start, latent_blocks, kv_blocks):
+def attend(flags, query_nope, query_rope, rel_start, rope_blocks, key_blocks, value_blocks):
     head_count, rows, _ = query_nope.shape
-    width = latent_blocks[0].shape[1]
-    blocks = len(latent_blocks)
+    blocks = len(rope_blocks)
     flops = head_count * blocks * rows * 2 * rows * (DN + DR + DV)
-    latent_spec = pl.BlockSpec((rows, width), lambda h, f: (0, 0))
-    kv_spec = pl.BlockSpec((rows, DN + DV), lambda h, f: (0, h))
+    rope_spec = pl.BlockSpec((DR, rows), lambda h, f: (0, 0))
+    key_spec = pl.BlockSpec((DN, rows), lambda h, f: (h, 0))
+    value_spec = pl.BlockSpec((rows, DV), lambda h, f: (0, h))
     return pl.pallas_call(
         attend_kernel,
         out_shape=jax.ShapeDtypeStruct((rows, head_count * DV), jnp.bfloat16),
@@ -114,8 +114,9 @@
                 pl.BlockSpec((1, rows, DR), lambda h, f: (h, 0, 0)),
                 pl.BlockSpec((rows, 1), lambda h, f: (0, 0)),
             ]
-            + [latent_spec] * blocks
-            + [kv_spec] * blocks,
+            + [rope_spec] * blocks
+            + [key_spec] * blocks
+            + [value_spec] * blocks,
             out_specs=pl.BlockSpec((rows, DV), lambda h, f: (0, h)),
             scratch_shapes=[
                 pltpu.VMEM((blocks, rows, DV), jnp.float32),
@@ -128,7 +129,7 @@
         cost_estimate=pl.CostEstimate(
             flops=flops, transcendentals=head_count * blocks * rows * rows, bytes_accessed=16 * 1024 * 1024
         ),
-    )(flags, query_nope, query_rope, rel_start, *latent_blocks, *kv_blocks)
+    )(flags, query_nope, query_rope, rel_start, *rope_blocks, *key_blocks, *value_blocks)
 
 
 def local(queries, latent_rope, doc_start, w_kv_up, w_out):
@@ -149,11 +150,19 @@
     key_last = block_first - distances * row_count + row_count - 1
     flags = (key_last >= lowest_start).astype(jnp.int32)
     latent_blocks = [held_at[d] for d in range(REACH + 1)]
-    kv_blocks = [
-        jnp.dot(block[:, :R], w_kv_up, preferred_element_type=jnp.float32).astype(jnp.bfloat16)
+    w_split = w_kv_up.reshape(R, head_count, 2, DN)
+    w_key = w_split[:, :, 0, :].reshape(R, head_count * DN)
+    w_value = w_split[:, :, 1, :].reshape(R, head_count * DV)
+    key_blocks = [
+        jnp.einsum("jr,rc->cj", block[:, :R], w_key, preferred_element_type=jnp.float32).astype(jnp.bfloat16)
         for block in latent_blocks
     ]
-    attended = attend(flags, query_nope, query_rope, rel_start, latent_blocks, kv_blocks)
+    value_blocks = [
+        jnp.dot(block[:, :R], w_value, preferred_element_type=jnp.float32).astype(jnp.bfloat16)
+        for block in latent_blocks
+    ]
+    rope_blocks = [block[:, R:].T for block in latent_blocks]
+    attended = attend(flags, query_nope, query_rope, rel_start, rope_blocks, key_blocks, value_blocks)
     return jnp.dot(attended, w_out, preferred_element_type=jnp.float32).astype(jnp.bfloat16)
 
 

time: 121 us -> 118 us (0.975)
  matrix products: 24.8 us -> 32.5 us
  Pallas kernels: 46.5 us -> 41.3 us
  waiting for transfers between devices: 17.4 us -> 13.1 us
  local copies, waits for them, and re-layouts: 10.3 us -> 13.5 us
  starting transfers between devices: 14.9 us -> 12.8 us
  other arithmetic: 5.29 us -> 3.52 us
    dot_general x8 -> x16, matrix products: 19.4 us -> 27.1 us  [the longest x8 13.9 us: local(): jnp.einsum('jr,rc->cj', block[:, :R], w_key, preferred_element_type=jnp.f...]
    pallas_call x1, Pallas kernels: 46.5 us -> 41.3 us  [attend(): pl.pallas_call(attend_kernel, out_shape=jax.ShapeDtypeStruct((rows, head_...]
    transpose x0 -> x7, local copies, waits for them, and re-layouts: none -> 5.16 us  [local(): rope_blocks = [block[:, R:].T for block in latent_blocks]]
    ppermute x9, waiting for transfers between devices: 17.4 us -> 13.1 us  [moved(): return lax.ppermute(value, 'srv', pairs)]
    ppermute x9, starting transfers between devices: 14.9 us -> 12.8 us  [moved(): return lax.ppermute(value, 'srv', pairs)]
    select_n x3, other arithmetic: 3.59 us -> 1.53 us  [odd_distance_block(): sent = jnp.where(upper_core, farther, nearer)]
  transfers between devices with their start and end apart: 9 -> 9, of which waited for: 3 -> 4; matrix products, arithmetic and copies ran while one was open for 24% -> 28% of each run, Pallas kernels for 0% -> 0%
where the time goes in v3:
time: 118 us; the launch traced here: 117 us
  Pallas kernels  41.3 us (35%)
  matrix products  32.5 us (28%)
  local copies, waits for them, and re-layouts  13.5 us (11%)
  waiting for transfers between devices  13.1 us (11%)
  starting transfers between devices  12.8 us (11%)
  other arithmetic  3.52 us (3%)
    pallas_call x1, Pallas kernels, attend(): pl.pallas_call(attend_kernel, out_shape=jax.ShapeDtypeStruct((rows, head_...  41.3 us
    dot_general x8, matrix products, local(): jnp.einsum('jr,rc->cj', block[:, :R], w_key, preferred_element_type=jnp.f...  13.9 us
    dot_general x8, matrix products, local(): jnp.dot(block[:, :R], w_value, preferred_element_type=jnp.float32)  13.2 us
    ppermute x9, waiting for transfers between devices, moved(): return lax.ppermute(value, 'srv', pairs)  13.1 us
    ppermute x9, starting transfers between devices, moved(): return lax.ppermute(value, 'srv', pairs)  12.8 us
    dot_general x1, matrix products, local(): jnp.dot(attended, w_out, preferred_element_type=jnp.float32)  5.37 us
    transpose x7, local copies, waits for them, and re-layouts, local(): rope_blocks = [block[:, R:].T for block in latent_blocks]  5.16 us
    unnamed x20, local copies, waits for them, and re-layouts  4.58 us
  transfers between devices with their start and end apart: 9, of which 4 were waited for; matrix products, arithmetic and copies ran while one was open for 28% of the time, Pallas kernels for 0%

profile of v3, /device:TPU:10, one launch (start us, length us, event | category | flops | bytes accessed | tf_op | source)
XLA Modules:
  0.0 116.8 jit_solution(14321312684818638338)
XLA Ops:
  0.0 1.3 %collective-permute-start.2 = (bf16[384,576]{0,1:T(8,128)(2,1)}, bf16[384,576]{0,1:T(8,128)(2,1)}, u32[]{:S(2)}, u32[]{:S(2)}) collective-permute-start(bf16[384,576]{0,1:T(8,128)(2,1)} %param.6), channel_id=1, source_target_pairs={{0,2},{1,3},{4,6},{5,7},{8,10},{9,11},{12,14},{13,15},{16,18},{17,... | collective-permute-start | bytes 1327112 | tf_op jit(solution)/shard_map/ppermute | solution.py:19
  1.3 3.5 %collective-permute-start = (bf16[384,576]{0,1:T(8,128)(2,1)}, bf16[384,576]{0,1:T(8,128)(2,1)}, u32[]{:S(2)}, u32[]{:S(2)}) collective-permute-start(bf16[384,576]{0,1:T(8,128)(2,1)} %param.6), channel_id=1, source_target_pairs={{0,4},{1,5},{2,6},{3,7},{4,8},{5,9},{6,10},{7,11},{8,12},{9,13},{1... | collective-permute-start | bytes 1327112 | tf_op jit(solution)/shard_map/ppermute | solution.py:19
  4.8 2.9 %copy.11 = bf16[512,2048]{0,1:T(8,128)(2,1)S(1)} copy(bf16[512,2048]{1,0:T(8,128)(2,1)} %param.8) | data formatting | bytes 4194304 | tf_op args[3]
  7.7 0.0 copy-start.5
  7.7 0.2 fusion.22
  7.9 0.0 copy-start.3
  7.9 0.0 copy-start.1
  7.9 0.0 copy-start.6
  7.9 0.9 copy-done.3
  8.9 0.0 copy-done.5
  8.9 1.6 %convolution_convert_fusion.16.rest_8_ = bf16[1024,384]{1,0:T(8,128)(2,1)} fusion(bf16[512,1024]{0,1:T(8,128)(2,1)S(1)} %bitcast.63, bf16[384,576]{0,1:T(8,128)(2,1)S(1)} %copy-done.5), kind=kOutput, calls=%fused_computation.16 | convolution fusion | flops 403046400 | bytes 2228224 | tf_op jit(solution)/shard_map/jr,rc->cj/dot_general | solution.py:157
  10.4 0.0 copy-done.6
  10.5 0.6 slice_bitcast_fusion.7.rest_0_
  11.1 1.5 %convolution_convert_fusion.14.rest_16_ = bf16[384,1024]{1,0:T(8,128)(2,1)} fusion(bf16[512,1024]{0,1:T(8,128)(2,1)S(1)} %bitcast.55, bf16[384,576]{0,1:T(8,128)(2,1)S(1)} %copy-done.6), kind=kOutput, calls=%fused_computation.14 | convolution fusion | flops 403046400 | bytes 2228224 | tf_op jit(solution)/shard_map/dot_general | solution.py:161
  12.6 2.8 %collective-permute-done = bf16[384,576]{0,1:T(8,128)(2,1)} collective-permute-done((bf16[384,576]{0,1:T(8,128)(2,1)}, bf16[384,576]{0,1:T(8,128)(2,1)}, u32[]{:S(2)}, u32[]{:S(2)}) %collective-permute-start) | collective-permute-done | bytes 442400 | tf_op jit(solution)/shard_map/ppermute | solution.py:19
  15.4 3.5 %collective-permute-start.5 = (bf16[384,576]{0,1:T(8,128)(2,1)}, bf16[384,576]{0,1:T(8,128)(2,1)S(1)}, u32[]{:S(2)}, u32[]{:S(2)}) collective-permute-start(bf16[384,576]{0,1:T(8,128)(2,1)} %collective-permute-done), channel_id=1, source_target_pairs={{1,5},{2,6},{3,7},{5,9},{6,10},{7,11},{9,13},{10,14},{11,15},{17,2... | collective-permute-start | bytes 1327112 | tf_op jit(solution)/shard_map/ppermute | solution.py:19
  18.9 0.7 broadcast_subtract_fusion
  19.6 0.7 copy.9
  20.4 0.7 copy.10
  21.1 0.0 copy-start.4
  21.1 1.0 slice.89.qr_ref
  22.1 1.0 slice.88.qn_ref
  23.1 0.8 reshape.12.rel_ref
  23.9 1.3 %compare_convert_fusion.flag_ref = s32[8]{0:T(128)} fusion(s32[]{:T(128)} %get-tuple-element.13, s32[]{:T(128)S(6)} %mul.6), kind=kLoop, calls=%fused_computation.53 | loop fusion | flops 40 | bytes 40 | tf_op jit(solution)/shard_map/convert_element_type | solution.py:151
  25.2 0.3 collective-permute-start.1
  25.5 2.6 %convolution_convert_fusion.15.rest_12_ = bf16[1024,384]{1,0:T(8,128)(2,1)} fusion(bf16[512,1024]{0,1:T(8,128)(2,1)S(1)} %bitcast.64, bf16[384,576]{0,1:T(8,128)(2,1)} %collective-permute-done), kind=kOutput, calls=%fused_computation.15 | convolution fusion | flops 403046400 | bytes 2228224 | tf_op jit(solution)/shard_map/jr,rc->cj/dot_general | solution.py:157
  28.1 0.4 collective-permute-done.5
  28.6 3.2 %collective-permute-start.6 = (bf16[384,576]{0,1:T(8,128)(2,1)S(1)}, bf16[384,576]{0,1:T(8,128)(2,1)S(1)}, u32[]{:S(2)}, u32[]{:S(2)}) collective-permute-start(bf16[384,576]{0,1:T(8,128)(2,1)S(1)} %collective-permute-done.5), channel_id=1, source_target_pairs={{2,0},{3,1},{6,4},{7,5},{10,8},{11,9},{14,12},{15,13},{18,16},{19,... | collective-permute-start | bytes 1327112 | tf_op jit(solution)/shard_map/ppermute | solution.py:19
  31.8 2.5 %convolution_convert_fusion.10.rest_20_ = bf16[384,1024]{1,0:T(8,128)(2,1)} fusion(bf16[512,1024]{0,1:T(8,128)(2,1)S(1)} %bitcast.56, bf16[384,576]{0,1:T(8,128)(2,1)} %collective-permute-done), kind=kOutput, calls=%fused_computation.10 | convolution fusion | flops 403046400 | bytes 2228224 | tf_op jit(solution)/shard_map/dot_general | solution.py:161
  34.3 1.4 %slice_bitcast_fusion.3.rest_4_ = bf16[64,384]{1,0:T(8,128)(2,1)} fusion(bf16[384,576]{0,1:T(8,128)(2,1)} %collective-permute-done), kind=kLoop, calls=%fused_computation.48 | loop fusion | bytes 98304 | tf_op jit(solution)/shard_map/transpose | solution.py:164
  35.7 1.6 %collective-permute-done.1 = bf16[384,576]{0,1:T(8,128)(2,1)S(1)} collective-permute-done((bf16[384,576]{0,1:T(8,128)(2,1)}, bf16[384,576]{0,1:T(8,128)(2,1)S(1)}, u32[]{:S(2)}, u32[]{:S(2)}) %collective-permute-start.1) | collective-permute-done | bytes 442400 | tf_op jit(solution)/shard_map/ppermute | solution.py:19
  37.3 8.2 %collective-permute-done.6 = bf16[384,576]{0,1:T(8,128)(2,1)S(1)} collective-permute-done((bf16[384,576]{0,1:T(8,128)(2,1)S(1)}, bf16[384,576]{0,1:T(8,128)(2,1)S(1)}, u32[]{:S(2)}, u32[]{:S(2)}) %collective-permute-start.6) | collective-permute-done | bytes 442400 | tf_op jit(solution)/shard_map/ppermute | solution.py:19
  45.5 0.1 broadcast_select_fusion.2
  45.6 0.0 copy-start.7
  45.6 0.0 collective-permute-done.2
  45.7 1.4 %broadcast_select_fusion.4 = (bf16[384,576]{0,1:T(8,128)(2,1)S(1)}, bf16[384,576]{0,1:T(8,128)(2,1)S(1)}, bf16[384,576]{0,1:T(8,128)(2,1)S(1)}) fusion(bf16[384,576]{0,1:T(8,128)(2,1)} %collective-permute-done, pred[]{:T(512)S(6)} %eq.12, bf16[384,576]{0,1:T(8,128)(2,1)S(1)} %collective-permute-done.1, bf16[384,576]{0,1:T(8,128)(2,1)} %collective-permute-done.2, ...), kind=kLoop, calls=%fused_computation.27 | loop fusion | flops 663552 | bytes 3096578 | tf_op jit(solution)/shard_map/jit(_where)/select_n | solution.py:40
  47.0 0.1 broadcast_select_fusion.5
  47.1 1.6 %fusion.1.rest_10_ = bf16[1024,384]{1,0:T(8,128)(2,1)} fusion(bf16[512,1024]{0,1:T(8,128)(2,1)S(1)} %bitcast.65, bf16[384,576]{0,1:T(8,128)(2,1)S(1)} %get-tuple-element.8), kind=kOutput, calls=%fused_computation.18 | convolution fusion | flops 403046400 | bytes 2228224 | tf_op jit(solution)/shard_map/jr,rc->cj/dot_general | solution.py:157
  48.7 1.5 %convolution_convert_fusion.12.rest_18_ = bf16[384,1024]{1,0:T(8,128)(2,1)} fusion(bf16[512,1024]{0,1:T(8,128)(2,1)S(1)} %bitcast.57, bf16[384,576]{0,1:T(8,128)(2,1)S(1)} %get-tuple-element.8), kind=kOutput, calls=%fused_computation.12 | convolution fusion | flops 403046400 | bytes 2228224 | tf_op jit(solution)/shard_map/dot_general | solution.py:161
  50.3 1.6 %fusion.4.rest_14_ = bf16[1024,384]{1,0:T(8,128)(2,1)} fusion(bf16[512,1024]{0,1:T(8,128)(2,1)S(1)} %bitcast.66, bf16[384,576]{0,1:T(8,128)(2,1)S(1)} %get-tuple-element.6), kind=kOutput, calls=%fused_computation.21 | convolution fusion | flops 403046400 | bytes 2228224 | tf_op jit(solution)/shard_map/jr,rc->cj/dot_general | solution.py:157
  51.9 0.4 collective-permute-start.3
  52.3 0.1 collective-permute-start.4
  52.4 0.4 collective-permute-start.7
  52.8 0.1 collective-permute-start.8
  52.9 0.6 slice_bitcast_fusion.1
  53.6 1.6 %convolution_convert_fusion.8.rest_22_ = bf16[384,1024]{1,0:T(8,128)(2,1)} fusion(bf16[512,1024]{0,1:T(8,128)(2,1)S(1)} %bitcast.58, bf16[384,576]{0,1:T(8,128)(2,1)S(1)} %get-tuple-element.6), kind=kOutput, calls=%fused_computation.8 | convolution fusion | flops 403046400 | bytes 2228224 | tf_op jit(solution)/shard_map/dot_general | solution.py:161
  55.1 0.0 collective-permute-done.3
  55.1 1.6 %fusion.rest_9_ = bf16[1024,384]{1,0:T(8,128)(2,1)} fusion(bf16[512,1024]{0,1:T(8,128)(2,1)S(1)} %bitcast.67, bf16[384,576]{0,1:T(8,128)(2,1)S(1)} %collective-permute-done.3), kind=kOutput, calls=%fused_computation.17 | convolution fusion | flops 403046400 | bytes 2228224 | tf_op jit(solution)/shard_map/jr,rc->cj/dot_general | solution.py:157
  56.7 0.6 slice_bitcast_fusion.6.rest_1_
  57.3 1.5 %convolution_convert_fusion.13.rest_17_ = bf16[384,1024]{1,0:T(8,128)(2,1)} fusion(bf16[512,1024]{0,1:T(8,128)(2,1)S(1)} %bitcast.59, bf16[384,576]{0,1:T(8,128)(2,1)S(1)} %collective-permute-done.3), kind=kOutput, calls=%fused_computation.13 | convolution fusion | flops 403046400 | bytes 2228224 | tf_op jit(solution)/shard_map/dot_general | solution.py:161
  58.8 0.0 collective-permute-done.4
  58.8 1.6 %fusion.2.rest_11_ = bf16[1024,384]{1,0:T(8,128)(2,1)} fusion(bf16[512,1024]{0,1:T(8,128)(2,1)S(1)} %bitcast.68, bf16[384,576]{0,1:T(8,128)(2,1)S(1)} %collective-permute-done.4), kind=kOutput, calls=%fused_computation.19 | convolution fusion | flops 403046400 | bytes 2228224 | tf_op jit(solution)/shard_map/jr,rc->cj/dot_general | solution.py:157
  60.4 0.6 slice_bitcast_fusion.4.rest_3_
  61.1 1.5 %convolution_convert_fusion.11.rest_19_ = bf16[384,1024]{1,0:T(8,128)(2,1)} fusion(bf16[512,1024]{0,1:T(8,128)(2,1)S(1)} %bitcast.60, bf16[384,576]{0,1:T(8,128)(2,1)S(1)} %collective-permute-done.4), kind=kOutput, calls=%fused_computation.11 | convolution fusion | flops 403046400 | bytes 2228224 | tf_op jit(solution)/shard_map/dot_general | solution.py:161
  62.6 0.0 collective-permute-done.7
  62.6 1.6 %fusion.3.rest_13_ = bf16[1024,384]{1,0:T(8,128)(2,1)} fusion(bf16[512,1024]{0,1:T(8,128)(2,1)S(1)} %bitcast.69, bf16[384,576]{0,1:T(8,128)(2,1)S(1)} %collective-permute-done.7), kind=kOutput, calls=%fused_computation.20 | convolution fusion | flops 403046400 | bytes 2228224 | tf_op jit(solution)/shard_map/jr,rc->cj/dot_general | solution.py:157
  64.2 0.6 slice_bitcast_fusion.2.rest_5_
  64.8 1.5 %convolution_convert_fusion.9.rest_21_ = bf16[384,1024]{1,0:T(8,128)(2,1)} fusion(bf16[512,1024]{0,1:T(8,128)(2,1)S(1)} %bitcast.61, bf16[384,576]{0,1:T(8,128)(2,1)S(1)} %collective-permute-done.7), kind=kOutput, calls=%fused_computation.9 | convolution fusion | flops 403046400 | bytes 2228224 | tf_op jit(solution)/shard_map/dot_general | solution.py:161
  66.3 0.0 collective-permute-done.8
  66.3 0.6 slice_bitcast_fusion.rest_7_
  66.9 1.6 %fusion.5.rest_15_ = bf16[1024,384]{1,0:T(8,128)(2,1)} fusion(bf16[512,1024]{0,1:T(8,128)(2,1)S(1)} %bitcast.70, bf16[384,576]{0,1:T(8,128)(2,1)S(1)} %collective-permute-done.8), kind=kOutput, calls=%fused_computation.22 | convolution fusion | flops 403046400 | bytes 2228224 | tf_op jit(solution)/shard_map/jr,rc->cj/dot_general | solution.py:157
  68.6 1.5 %convolution_convert_fusion.7.rest_23_ = bf16[384,1024]{1,0:T(8,128)(2,1)} fusion(bf16[512,1024]{0,1:T(8,128)(2,1)S(1)} %bitcast.62, bf16[384,576]{0,1:T(8,128)(2,1)S(1)} %collective-permute-done.8), kind=kOutput, calls=%fused_computation.7 | convolution fusion | flops 403046400 | bytes 2228224 | tf_op jit(solution)/shard_map/dot_general | solution.py:161
  70.1 41.3 %shard_map.55 = bf16[384,1024]{1,0:T(8,128)(2,1)} custom-call(s32[8]{0:T(128)} %compare_convert_fusion.flag_ref, bf16[8,384,128]{2,1,0:T(8,128)(2,1)} %slice.88.qn_ref, bf16[8,384,64]{2,1,0:T(8,128)(2,1)} %slice.89.qr_ref, s32[384,1]{1,0:T(8,128)} %reshape.12.rel_ref, bf16[64,384]{1,0:T(8,128)(2,1)} %slice_bitcast_fusion.7.rest_0_, ...), custom_call_target="tpu_custom_call" | custom-call | flops 6039797760 | bytes 16777216 | tf_op jit(solution)/shard_map/pallas_call | solution.py:106
  111.5 5.4 %convolution_convert_fusion = bf16[384,2048]{1,0:T(8,128)(2,1)} fusion(bf16[384,1024]{1,0:T(8,128)(2,1)} %shard_map.55, bf16[1024,2048]{1,0:T(8,128)(2,1)} %param.9), kind=kOutput, calls=%fused_computation | convolution fusion | flops 1611399168 | bytes 6553600 | tf_op jit(solution)/shard_map/dot_general | solution.py:166
  (9 shorter events, 0.0 us)
Async XLA Ops:
  0.0 45.6 %collective-permute-start.2 = (bf16[384,576]{0,1:T(8,128)(2,1)}, bf16[384,576]{0,1:T(8,128)(2,1)}, u32[]{:S(2)}, u32[]{:S(2)}) collective-permute-start(bf16[384,576]{0,1:T(8,128)(2,1)} %param.6), channel_id=1, source_target_pairs={{0,2},{1,3},{4,6},{5,7},{8,10},{9,11},{12,14},{13,15},{16,18},{17,... | collective-permute-start | bytes 1327112 | tf_op jit(solution)/shard_map/ppermute | solution.py:19
  1.3 14.1 %collective-permute-start = (bf16[384,576]{0,1:T(8,128)(2,1)}, bf16[384,576]{0,1:T(8,128)(2,1)}, u32[]{:S(2)}, u32[]{:S(2)}) collective-permute-start(bf16[384,576]{0,1:T(8,128)(2,1)} %param.6), channel_id=1, source_target_pairs={{0,4},{1,5},{2,6},{3,7},{4,8},{5,9},{6,10},{7,11},{8,12},{9,13},{1... | collective-permute-start | bytes 1327112 | tf_op jit(solution)/shard_map/ppermute | solution.py:19
  7.7 1.2 %copy-start.5 = (bf16[384,576]{0,1:T(8,128)(2,1)S(1)}, bf16[384,576]{0,1:T(8,128)(2,1)}, u32[]{:S(2)}) copy-start(bf16[384,576]{0,1:T(8,128)(2,1)} %param.6) | copy-start | bytes 1327108
  7.9 1.0 copy-start.3
  7.9 4.7 %copy-start.1 = (bf16[512,8,1,128]{0,3,2,1:T(8,128)(2,1)}, bf16[512,8,1,128]{0,3,2,1:T(8,128)(2,1)S(1)}, u32[]{:S(2)}) copy-start(bf16[512,8,1,128]{0,3,2,1:T(8,128)(2,1)S(1)} %get-tuple-element.9) | copy-start | bytes 3145732
  7.9 2.5 %copy-start.6 = (bf16[384,576]{0,1:T(8,128)(2,1)S(1)}, bf16[384,576]{0,1:T(8,128)(2,1)}, u32[]{:S(2)}) copy-start(bf16[384,576]{0,1:T(8,128)(2,1)} %param.6) | copy-start | bytes 1327108
  10.4 8.4 %copy-start.8 = (s32[384]{0:T(512)S(1)}, s32[384]{0:T(512)}, u32[]{:S(2)}) copy-start(s32[384]{0:T(512)} %param.7) | copy-start | bytes 4612
  10.4 9.2 %copy-start = (bf16[384,1536]{1,0:T(8,128)(2,1)S(1)}, bf16[384,1536]{1,0:T(8,128)(2,1)}, u32[]{:S(2)}) copy-start(bf16[384,1536]{1,0:T(8,128)(2,1)} %param.5) | copy-start | bytes 3538948
  15.4 13.1 %collective-permute-start.5 = (bf16[384,576]{0,1:T(8,128)(2,1)}, bf16[384,576]{0,1:T(8,128)(2,1)S(1)}, u32[]{:S(2)}, u32[]{:S(2)}) collective-permute-start(bf16[384,576]{0,1:T(8,128)(2,1)} %collective-permute-done), channel_id=1, source_target_pairs={{1,5},{2,6},{3,7},{5,9},{6,10},{7,11},{9,13},{10,14},{11,15},{17,2... | collective-permute-start | bytes 1327112 | tf_op jit(solution)/shard_map/ppermute | solution.py:19
  21.1 4.4 %copy-start.4 = (bf16[512,8,1,128]{0,3,2,1:T(8,128)(2,1)S(1)}, bf16[512,8,1,128]{0,3,2,1:T(8,128)(2,1)}, u32[]{:S(2)}) copy-start(bf16[512,8,1,128]{0,3,2,1:T(8,128)(2,1)} %copy-done.3) | copy-start | bytes 3145732
  23.1 8.6 %copy-start.2 = (bf16[512,8,1,128]{0,3,2,1:T(8,128)(2,1)S(1)}, bf16[512,8,1,128]{0,3,2,1:T(8,128)(2,1)}, u32[]{:S(2)}) copy-start(bf16[512,8,1,128]{0,3,2,1:T(8,128)(2,1)} %copy-done.1) | copy-start | bytes 3145732
  25.2 12.1 %collective-permute-start.1 = (bf16[384,576]{0,1:T(8,128)(2,1)}, bf16[384,576]{0,1:T(8,128)(2,1)S(1)}, u32[]{:S(2)}, u32[]{:S(2)}) collective-permute-start(bf16[384,576]{0,1:T(8,128)(2,1)} %collective-permute-done), channel_id=1, source_target_pairs={{0,2},{1,3},{2,0},{3,1},{4,6},{5,7},{6,4},{7,5},{8,10},{9,11},{10,... | collective-permute-start | bytes 1327112 | tf_op jit(solution)/shard_map/ppermute | solution.py:19
  28.6 17.0 %collective-permute-start.6 = (bf16[384,576]{0,1:T(8,128)(2,1)S(1)}, bf16[384,576]{0,1:T(8,128)(2,1)S(1)}, u32[]{:S(2)}, u32[]{:S(2)}) collective-permute-start(bf16[384,576]{0,1:T(8,128)(2,1)S(1)} %collective-permute-done.5), channel_id=1, source_target_pairs={{2,0},{3,1},{6,4},{7,5},{10,8},{11,9},{14,12},{15,13},{18,16},{19,... | collective-permute-start | bytes 1327112 | tf_op jit(solution)/shard_map/ppermute | solution.py:19
  45.6 1.4 %copy-start.7 = (bf16[384,576]{0,1:T(8,128)(2,1)S(1)}, bf16[384,576]{0,1:T(8,128)(2,1)}, u32[]{:S(2)}) copy-start(bf16[384,576]{0,1:T(8,128)(2,1)} %param.6) | copy-start | bytes 1327108
  51.9 3.2 %collective-permute-start.3 = (bf16[384,576]{0,1:T(8,128)(2,1)S(1)}, bf16[384,576]{0,1:T(8,128)(2,1)S(1)}, u32[]{:S(2)}, u32[]{:S(2)}) collective-permute-start(bf16[384,576]{0,1:T(8,128)(2,1)S(1)} %broadcast_select_fusion.5), channel_id=1, source_target_pairs={{0,1},{1,0},{2,3},{3,2},{4,5},{5,4},{6,7},{7,6},{8,9},{9,8},{10,11... | collective-permute-start | bytes 1327112 | tf_op jit(solution)/shard_map/ppermute | solution.py:19
  52.3 6.6 %collective-permute-start.4 = (bf16[384,576]{0,1:T(8,128)(2,1)S(1)}, bf16[384,576]{0,1:T(8,128)(2,1)S(1)}, u32[]{:S(2)}, u32[]{:S(2)}) collective-permute-start(bf16[384,576]{0,1:T(8,128)(2,1)S(1)} %get-tuple-element.7), channel_id=1, source_target_pairs={{0,1},{1,0},{2,3},{3,2},{4,5},{5,4},{6,7},{7,6},{8,9},{9,8},{10,11... | collective-permute-start | bytes 1327112 | tf_op jit(solution)/shard_map/ppermute | solution.py:19
  52.4 10.2 %collective-permute-start.7 = (bf16[384,576]{0,1:T(8,128)(2,1)S(1)}, bf16[384,576]{0,1:T(8,128)(2,1)S(1)}, u32[]{:S(2)}, u32[]{:S(2)}) collective-permute-start(bf16[384,576]{0,1:T(8,128)(2,1)S(1)} %get-tuple-element.11), channel_id=1, source_target_pairs={{0,1},{1,0},{2,3},{3,2},{4,5},{5,4},{6,7},{7,6},{8,9},{9,8},{10,11... | collective-permute-start | bytes 1327112 | tf_op jit(solution)/shard_map/ppermute | solution.py:19
  52.8 13.5 %collective-permute-start.8 = (bf16[384,576]{0,1:T(8,128)(2,1)S(1)}, bf16[384,576]{0,1:T(8,128)(2,1)S(1)}, u32[]{:S(2)}, u32[]{:S(2)}) collective-permute-start(bf16[384,576]{0,1:T(8,128)(2,1)S(1)} %get-tuple-element.5), channel_id=1, source_target_pairs={{0,1},{1,0},{2,3},{3,2},{4,5},{5,4},{6,7},{7,6},{8,9},{9,8},{10,11... | collective-permute-start | bytes 1327112 | tf_op jit(solution)/shard_map/ppermute | solution.py:19

commit v4 on v3

--- a/solution.py
+++ b/solution.py
@@ -153,6 +153,7 @@
     w_split = w_kv_up.reshape(R, head_count, 2, DN)
     w_key = w_split[:, :, 0, :].reshape(R, head_count * DN)
     w_value = w_split[:, :, 1, :].reshape(R, head_count * DV)
+    w_key, w_value = lax.optimization_barrier((w_key, w_value))
     key_blocks = [
         jnp.einsum("jr,rc->cj", block[:, :R], w_key, preferred_element_type=jnp.float32).astype(jnp.bfloat16)
         for block in latent_blocks

time: 118 us -> 118 us (level)
  transfers between devices with their start and end apart: 9 -> 9, of which waited for: 4 -> 5; matrix products, arithmetic and copies ran while one was open for 28% -> 31% of each run, Pallas kernels for 0% -> 0%
where the time goes in v4:
time: 118 us; the launch traced here: 117 us
  Pallas kernels  41.3 us (35%)
  matrix products  32.4 us (27%)
  local copies, waits for them, and re-layouts  13.5 us (11%)
  waiting for transfers between devices  13.5 us (11%)
  starting transfers between devices  12.8 us (11%)
  other arithmetic  3.53 us (3%)
    pallas_call x1, Pallas kernels, attend(): pl.pallas_call(attend_kernel, out_shape=jax.ShapeDtypeStruct((rows, head_...  41.3 us
    dot_general x8, matrix products, local(): jnp.einsum('jr,rc->cj', block[:, :R], w_key, preferred_element_type=jnp.f...  13.8 us
    ppermute x9, waiting for transfers between devices, moved(): return lax.ppermute(value, 'srv', pairs)  13.5 us
    dot_general x8, matrix products, local(): jnp.dot(block[:, :R], w_value, preferred_element_type=jnp.float32)  13.3 us
    ppermute x9, starting transfers between devices, moved(): return lax.ppermute(value, 'srv', pairs)  12.8 us
    dot_general x1, matrix products, local(): jnp.dot(attended, w_out, preferred_element_type=jnp.float32)  5.37 us
    transpose x7, local copies, waits for them, and re-layouts, local(): rope_blocks = [block[:, R:].T for block in latent_blocks]  5.17 us
    unnamed x20, local copies, waits for them, and re-layouts  4.58 us
  transfers between devices with their start and end apart: 9, of which 5 were waited for; matrix products, arithmetic and copies ran while one was open for 31% of the time, Pallas kernels for 0%

profile of v4, /device:TPU:10, one launch (start us, length us, event | category | flops | bytes accessed | tf_op | source)
XLA Modules:
  0.0 117.3 jit_solution(17654923888639793644)
XLA Ops:
  0.0 1.3 %collective-permute-start.2 = (bf16[384,576]{0,1:T(8,128)(2,1)}, bf16[384,576]{0,1:T(8,128)(2,1)}, u32[]{:S(2)}, u32[]{:S(2)}) collective-permute-start(bf16[384,576]{0,1:T(8,128)(2,1)} %param.6), channel_id=1, source_target_pairs={{0,2},{1,3},{4,6},{5,7},{8,10},{9,11},{12,14},{13,15},{16,18},{17,... | collective-permute-start | bytes 1327112 | tf_op jit(solution)/shard_map/ppermute | solution.py:19
  1.3 3.5 %collective-permute-start = (bf16[384,576]{0,1:T(8,128)(2,1)}, bf16[384,576]{0,1:T(8,128)(2,1)}, u32[]{:S(2)}, u32[]{:S(2)}) collective-permute-start(bf16[384,576]{0,1:T(8,128)(2,1)} %param.6), channel_id=1, source_target_pairs={{0,4},{1,5},{2,6},{3,7},{4,8},{5,9},{6,10},{7,11},{8,12},{9,13},{1... | collective-permute-start | bytes 1327112 | tf_op jit(solution)/shard_map/ppermute | solution.py:19
  4.8 2.9 %copy.11 = bf16[512,2048]{0,1:T(8,128)(2,1)S(1)} copy(bf16[512,2048]{1,0:T(8,128)(2,1)} %param.8) | data formatting | bytes 4194304 | tf_op args[3]
  7.7 0.0 copy-start.5
  7.7 0.2 fusion.18
  7.9 0.0 copy-start.3
  7.9 0.0 copy-start.1
  7.9 0.0 copy-start.6
  7.9 0.9 copy-done.3
  8.9 0.0 copy-done.5
  8.9 1.6 %convolution_convert_fusion.16.rest_8_ = bf16[1024,384]{1,0:T(8,128)(2,1)} fusion(bf16[512,1024]{0,1:T(8,128)(2,1)S(1)} %bitcast.55, bf16[384,576]{0,1:T(8,128)(2,1)S(1)} %copy-done.5), kind=kOutput, calls=%fused_computation.16 | convolution fusion | flops 403046400 | bytes 2228224 | tf_op jit(solution)/shard_map/jr,rc->cj/dot_general | solution.py:158
  10.5 0.6 slice_bitcast_fusion.7.rest_0_
  11.1 1.5 %fusion.rest_16_ = bf16[384,1024]{1,0:T(8,128)(2,1)} fusion(bf16[512,1024]{0,1:T(8,128)(2,1)S(1)} %bitcast.47, bf16[384,576]{0,1:T(8,128)(2,1)S(1)} %copy-done.6), kind=kOutput, calls=%fused_computation.17 | convolution fusion | flops 403046400 | bytes 2228224 | tf_op jit(solution)/shard_map/dot_general | solution.py:162
  12.6 2.8 %collective-permute-done = bf16[384,576]{0,1:T(8,128)(2,1)} collective-permute-done((bf16[384,576]{0,1:T(8,128)(2,1)}, bf16[384,576]{0,1:T(8,128)(2,1)}, u32[]{:S(2)}, u32[]{:S(2)}) %collective-permute-start) | collective-permute-done | bytes 442400 | tf_op jit(solution)/shard_map/ppermute | solution.py:19
  15.4 3.5 %collective-permute-start.5 = (bf16[384,576]{0,1:T(8,128)(2,1)}, bf16[384,576]{0,1:T(8,128)(2,1)S(1)}, u32[]{:S(2)}, u32[]{:S(2)}) collective-permute-start(bf16[384,576]{0,1:T(8,128)(2,1)} %collective-permute-done), channel_id=1, source_target_pairs={{1,5},{2,6},{3,7},{5,9},{6,10},{7,11},{9,13},{10,14},{11,15},{17,2... | collective-permute-start | bytes 1327112 | tf_op jit(solution)/shard_map/ppermute | solution.py:19
  18.9 0.7 broadcast_subtract_fusion
  19.6 0.0 copy-done
  19.6 0.7 copy.9
  20.4 0.7 copy.10
  21.1 0.0 copy-start.4
  21.1 1.0 slice.89.qr_ref
  22.1 1.0 slice.88.qn_ref
  23.1 0.8 reshape.12.rel_ref
  23.9 1.3 %compare_convert_fusion.flag_ref = s32[8]{0:T(128)} fusion(s32[]{:T(128)} %get-tuple-element.17, s32[]{:T(128)S(6)} %mul.6), kind=kLoop, calls=%fused_computation.49 | loop fusion | flops 40 | bytes 40 | tf_op jit(solution)/shard_map/convert_element_type | solution.py:151
  25.2 0.3 collective-permute-start.1
  25.5 2.6 %convolution_convert_fusion.12.rest_12_ = bf16[1024,384]{1,0:T(8,128)(2,1)} fusion(bf16[512,1024]{0,1:T(8,128)(2,1)S(1)} %bitcast.56, bf16[384,576]{0,1:T(8,128)(2,1)} %collective-permute-done), kind=kOutput, calls=%fused_computation.12 | convolution fusion | flops 403046400 | bytes 2228224 | tf_op jit(solution)/shard_map/jr,rc->cj/dot_general | solution.py:158
  28.1 0.4 collective-permute-done.5
  28.6 3.2 %collective-permute-start.6 = (bf16[384,576]{0,1:T(8,128)(2,1)S(1)}, bf16[384,576]{0,1:T(8,128)(2,1)S(1)}, u32[]{:S(2)}, u32[]{:S(2)}) collective-permute-start(bf16[384,576]{0,1:T(8,128)(2,1)S(1)} %collective-permute-done.5), channel_id=1, source_target_pairs={{2,0},{3,1},{6,4},{7,5},{10,8},{11,9},{14,12},{15,13},{18,16},{19,... | collective-permute-start | bytes 1327112 | tf_op jit(solution)/shard_map/ppermute | solution.py:19
  31.8 1.4 %slice_bitcast_fusion.3.rest_4_ = bf16[64,384]{1,0:T(8,128)(2,1)} fusion(bf16[384,576]{0,1:T(8,128)(2,1)} %collective-permute-done), kind=kLoop, calls=%fused_computation.44 | loop fusion | bytes 98304 | tf_op jit(solution)/shard_map/transpose | solution.py:165
  33.2 0.0 copy-done.2
  33.2 2.5 %fusion.1.rest_20_ = bf16[384,1024]{1,0:T(8,128)(2,1)} fusion(bf16[512,1024]{0,1:T(8,128)(2,1)S(1)} %bitcast.48, bf16[384,576]{0,1:T(8,128)(2,1)} %collective-permute-done), kind=kOutput, calls=%fused_computation.18 | convolution fusion | flops 403046400 | bytes 2228224 | tf_op jit(solution)/shard_map/dot_general | solution.py:162
  35.7 1.5 %collective-permute-done.1 = bf16[384,576]{0,1:T(8,128)(2,1)S(1)} collective-permute-done((bf16[384,576]{0,1:T(8,128)(2,1)}, bf16[384,576]{0,1:T(8,128)(2,1)S(1)}, u32[]{:S(2)}, u32[]{:S(2)}) %collective-permute-start.1) | collective-permute-done | bytes 442400 | tf_op jit(solution)/shard_map/ppermute | solution.py:19
  37.3 8.2 %collective-permute-done.6 = bf16[384,576]{0,1:T(8,128)(2,1)S(1)} collective-permute-done((bf16[384,576]{0,1:T(8,128)(2,1)S(1)}, bf16[384,576]{0,1:T(8,128)(2,1)S(1)}, u32[]{:S(2)}, u32[]{:S(2)}) %collective-permute-start.6) | collective-permute-done | bytes 442400 | tf_op jit(solution)/shard_map/ppermute | solution.py:19
  45.5 0.1 broadcast_select_fusion.2
  45.6 1.6 %convolution_convert_fusion.10.rest_14_ = bf16[1024,384]{1,0:T(8,128)(2,1)} fusion(bf16[512,1024]{0,1:T(8,128)(2,1)S(1)} %bitcast.57, bf16[384,576]{0,1:T(8,128)(2,1)S(1)} %get-tuple-element.10), kind=kOutput, calls=%fused_computation.10 | convolution fusion | flops 403046400 | bytes 2228224 | tf_op jit(solution)/shard_map/jr,rc->cj/dot_general | solution.py:158
  47.2 1.5 %convolution_convert_fusion.2.rest_22_ = bf16[384,1024]{1,0:T(8,128)(2,1)} fusion(bf16[512,1024]{0,1:T(8,128)(2,1)S(1)} %bitcast.49, bf16[384,576]{0,1:T(8,128)(2,1)S(1)} %get-tuple-element.10), kind=kOutput, calls=%fused_computation.2 | convolution fusion | flops 403046400 | bytes 2228224 | tf_op jit(solution)/shard_map/dot_general | solution.py:162
  48.8 0.0 collective-permute-done.2
  48.8 1.4 %broadcast_select_fusion.4 = (bf16[384,576]{0,1:T(8,128)(2,1)S(1)}, bf16[384,576]{0,1:T(8,128)(2,1)S(1)}, bf16[384,576]{0,1:T(8,128)(2,1)S(1)}) fusion(bf16[384,576]{0,1:T(8,128)(2,1)} %collective-permute-done, pred[]{:T(512)S(6)} %eq.12, bf16[384,576]{0,1:T(8,128)(2,1)S(1)} %collective-permute-done.1, bf16[384,576]{0,1:T(8,128)(2,1)} %collective-permute-done.2, ...), kind=kLoop, calls=%fused_computation.23 | loop fusion | flops 663552 | bytes 3096578 | tf_op jit(solution)/shard_map/jit(_where)/select_n | solution.py:40
  50.1 0.1 broadcast_select_fusion.5
  50.2 1.6 %convolution_convert_fusion.14.rest_10_ = bf16[1024,384]{1,0:T(8,128)(2,1)} fusion(bf16[512,1024]{0,1:T(8,128)(2,1)S(1)} %bitcast.58, bf16[384,576]{0,1:T(8,128)(2,1)S(1)} %get-tuple-element.12), kind=kOutput, calls=%fused_computation.14 | convolution fusion | flops 403046400 | bytes 2228224 | tf_op jit(solution)/shard_map/jr,rc->cj/dot_general | solution.py:158
  51.8 0.4 collective-permute-start.3
  52.2 0.1 collective-permute-start.4
  52.3 0.4 collective-permute-start.7
  52.7 0.1 collective-permute-start.8
  52.8 0.6 slice_bitcast_fusion.1
  53.5 1.5 %convolution_convert_fusion.6.rest_18_ = bf16[384,1024]{1,0:T(8,128)(2,1)} fusion(bf16[512,1024]{0,1:T(8,128)(2,1)S(1)} %bitcast.50, bf16[384,576]{0,1:T(8,128)(2,1)S(1)} %get-tuple-element.12), kind=kOutput, calls=%fused_computation.6 | convolution fusion | flops 403046400 | bytes 2228224 | tf_op jit(solution)/shard_map/dot_general | solution.py:162
  55.0 0.5 collective-permute-done.8
  55.5 1.6 %convolution_convert_fusion.9.rest_15_ = bf16[1024,384]{1,0:T(8,128)(2,1)} fusion(bf16[512,1024]{0,1:T(8,128)(2,1)S(1)} %bitcast.59, bf16[384,576]{0,1:T(8,128)(2,1)S(1)} %collective-permute-done.8), kind=kOutput, calls=%fused_computation.9 | convolution fusion | flops 403046400 | bytes 2228224 | tf_op jit(solution)/shard_map/jr,rc->cj/dot_general | solution.py:158
  57.1 1.5 %convolution_convert_fusion.1.rest_23_ = bf16[384,1024]{1,0:T(8,128)(2,1)} fusion(bf16[512,1024]{0,1:T(8,128)(2,1)S(1)} %bitcast.51, bf16[384,576]{0,1:T(8,128)(2,1)S(1)} %collective-permute-done.8), kind=kOutput, calls=%fused_computation.1 | convolution fusion | flops 403046400 | bytes 2228224 | tf_op jit(solution)/shard_map/dot_general | solution.py:162
  58.6 0.0 collective-permute-done.7
  58.6 1.6 %convolution_convert_fusion.11.rest_13_ = bf16[1024,384]{1,0:T(8,128)(2,1)} fusion(bf16[512,1024]{0,1:T(8,128)(2,1)S(1)} %bitcast.60, bf16[384,576]{0,1:T(8,128)(2,1)S(1)} %collective-permute-done.7), kind=kOutput, calls=%fused_computation.11 | convolution fusion | flops 403046400 | bytes 2228224 | tf_op jit(solution)/shard_map/jr,rc->cj/dot_general | solution.py:158
  60.2 0.6 slice_bitcast_fusion.2.rest_5_
  60.9 1.5 %convolution_convert_fusion.3.rest_21_ = bf16[384,1024]{1,0:T(8,128)(2,1)} fusion(bf16[512,1024]{0,1:T(8,128)(2,1)S(1)} %bitcast.52, bf16[384,576]{0,1:T(8,128)(2,1)S(1)} %collective-permute-done.7), kind=kOutput, calls=%fused_computation.3 | convolution fusion | flops 403046400 | bytes 2228224 | tf_op jit(solution)/shard_map/dot_general | solution.py:162
  62.4 0.0 collective-permute-done.4
  62.4 0.6 slice_bitcast_fusion.4.rest_3_
  63.0 1.6 %convolution_convert_fusion.13.rest_11_ = bf16[1024,384]{1,0:T(8,128)(2,1)} fusion(bf16[512,1024]{0,1:T(8,128)(2,1)S(1)} %bitcast.61, bf16[384,576]{0,1:T(8,128)(2,1)S(1)} %collective-permute-done.4), kind=kOutput, calls=%fused_computation.13 | convolution fusion | flops 403046400 | bytes 2228224 | tf_op jit(solution)/shard_map/jr,rc->cj/dot_general | solution.py:158
  64.7 0.6 slice_bitcast_fusion.rest_7_
  65.3 1.5 %convolution_convert_fusion.5.rest_19_ = bf16[384,1024]{1,0:T(8,128)(2,1)} fusion(bf16[512,1024]{0,1:T(8,128)(2,1)S(1)} %bitcast.53, bf16[384,576]{0,1:T(8,128)(2,1)S(1)} %collective-permute-done.4), kind=kOutput, calls=%fused_computation.5 | convolution fusion | flops 403046400 | bytes 2228224 | tf_op jit(solution)/shard_map/dot_general | solution.py:162
  66.8 0.0 collective-permute-done.3
  66.8 0.6 slice_bitcast_fusion.6.rest_1_
  67.4 1.6 %convolution_convert_fusion.15.rest_9_ = bf16[1024,384]{1,0:T(8,128)(2,1)} fusion(bf16[512,1024]{0,1:T(8,128)(2,1)S(1)} %bitcast.62, bf16[384,576]{0,1:T(8,128)(2,1)S(1)} %collective-permute-done.3), kind=kOutput, calls=%fused_computation.15 | convolution fusion | flops 403046400 | bytes 2228224 | tf_op jit(solution)/shard_map/jr,rc->cj/dot_general | solution.py:158
  69.0 1.5 %convolution_convert_fusion.7.rest_17_ = bf16[384,1024]{1,0:T(8,128)(2,1)} fusion(bf16[512,1024]{0,1:T(8,128)(2,1)S(1)} %bitcast.54, bf16[384,576]{0,1:T(8,128)(2,1)S(1)} %collective-permute-done.3), kind=kOutput, calls=%fused_computation.7 | convolution fusion | flops 403046400 | bytes 2228224 | tf_op jit(solution)/shard_map/dot_general | solution.py:162
  70.5 41.3 %shard_map.55 = bf16[384,1024]{1,0:T(8,128)(2,1)} custom-call(s32[8]{0:T(128)} %compare_convert_fusion.flag_ref, bf16[8,384,128]{2,1,0:T(8,128)(2,1)} %slice.88.qn_ref, bf16[8,384,64]{2,1,0:T(8,128)(2,1)} %slice.89.qr_ref, s32[384,1]{1,0:T(8,128)} %reshape.12.rel_ref, bf16[64,384]{1,0:T(8,128)(2,1)} %slice_bitcast_fusion.7.rest_0_, ...), custom_call_target="tpu_custom_call" | custom-call | flops 6039797760 | bytes 16777216 | tf_op jit(solution)/shard_map/pallas_call | solution.py:106
  111.9 5.4 %convolution_convert_fusion = bf16[384,2048]{1,0:T(8,128)(2,1)} fusion(bf16[384,1024]{1,0:T(8,128)(2,1)} %shard_map.55, bf16[1024,2048]{1,0:T(8,128)(2,1)} %param.9), kind=kOutput, calls=%fused_computation | convolution fusion | flops 1611399168 | bytes 6553600 | tf_op jit(solution)/shard_map/dot_general | solution.py:167
  (9 shorter events, 0.0 us)
Async XLA Ops:
  0.0 48.8 %collective-permute-start.2 = (bf16[384,576]{0,1:T(8,128)(2,1)}, bf16[384,576]{0,1:T(8,128)(2,1)}, u32[]{:S(2)}, u32[]{:S(2)}) collective-permute-start(bf16[384,576]{0,1:T(8,128)(2,1)} %param.6), channel_id=1, source_target_pairs={{0,2},{1,3},{4,6},{5,7},{8,10},{9,11},{12,14},{13,15},{16,18},{17,... | collective-permute-start | bytes 1327112 | tf_op jit(solution)/shard_map/ppermute | solution.py:19
  1.3 14.1 %collective-permute-start = (bf16[384,576]{0,1:T(8,128)(2,1)}, bf16[384,576]{0,1:T(8,128)(2,1)}, u32[]{:S(2)}, u32[]{:S(2)}) collective-permute-start(bf16[384,576]{0,1:T(8,128)(2,1)} %param.6), channel_id=1, source_target_pairs={{0,4},{1,5},{2,6},{3,7},{4,8},{5,9},{6,10},{7,11},{8,12},{9,13},{1... | collective-permute-start | bytes 1327112 | tf_op jit(solution)/shard_map/ppermute | solution.py:19
  7.7 1.2 %copy-start.5 = (bf16[384,576]{0,1:T(8,128)(2,1)S(1)}, bf16[384,576]{0,1:T(8,128)(2,1)}, u32[]{:S(2)}) copy-start(bf16[384,576]{0,1:T(8,128)(2,1)} %param.6) | copy-start | bytes 1327108
  7.9 1.0 copy-start.3
  7.9 4.7 %copy-start.1 = (bf16[512,8,1,128]{0,3,2,1:T(8,128)(2,1)}, bf16[512,8,1,128]{0,3,2,1:T(8,128)(2,1)S(1)}, u32[]{:S(2)}) copy-start(bf16[512,8,1,128]{0,3,2,1:T(8,128)(2,1)S(1)} %get-tuple-element.13) | copy-start | bytes 3145732
  7.9 2.5 %copy-start.6 = (bf16[384,576]{0,1:T(8,128)(2,1)S(1)}, bf16[384,576]{0,1:T(8,128)(2,1)}, u32[]{:S(2)}) copy-start(bf16[384,576]{0,1:T(8,128)(2,1)} %param.6) | copy-start | bytes 1327108
  10.4 8.4 %copy-start.8 = (s32[384]{0:T(512)S(1)}, s32[384]{0:T(512)}, u32[]{:S(2)}) copy-start(s32[384]{0:T(512)} %param.7) | copy-start | bytes 4612
  10.4 9.2 %copy-start = (bf16[384,1536]{1,0:T(8,128)(2,1)S(1)}, bf16[384,1536]{1,0:T(8,128)(2,1)}, u32[]{:S(2)}) copy-start(bf16[384,1536]{1,0:T(8,128)(2,1)} %param.5) | copy-start | bytes 3538948
  15.4 13.1 %collective-permute-start.5 = (bf16[384,576]{0,1:T(8,128)(2,1)}, bf16[384,576]{0,1:T(8,128)(2,1)S(1)}, u32[]{:S(2)}, u32[]{:S(2)}) collective-permute-start(bf16[384,576]{0,1:T(8,128)(2,1)} %collective-permute-done), channel_id=1, source_target_pairs={{1,5},{2,6},{3,7},{5,9},{6,10},{7,11},{9,13},{10,14},{11,15},{17,2... | collective-permute-start | bytes 1327112 | tf_op jit(solution)/shard_map/ppermute | solution.py:19
  21.1 4.4 %copy-start.4 = (bf16[512,8,1,128]{0,3,2,1:T(8,128)(2,1)S(1)}, bf16[512,8,1,128]{0,3,2,1:T(8,128)(2,1)}, u32[]{:S(2)}) copy-start(bf16[512,8,1,128]{0,3,2,1:T(8,128)(2,1)} %copy-done.3) | copy-start | bytes 3145732
  23.1 10.0 %copy-start.2 = (bf16[512,8,1,128]{0,3,2,1:T(8,128)(2,1)S(1)}, bf16[512,8,1,128]{0,3,2,1:T(8,128)(2,1)}, u32[]{:S(2)}) copy-start(bf16[512,8,1,128]{0,3,2,1:T(8,128)(2,1)} %copy-done.1) | copy-start | bytes 3145732
  25.2 12.1 %collective-permute-start.1 = (bf16[384,576]{0,1:T(8,128)(2,1)}, bf16[384,576]{0,1:T(8,128)(2,1)S(1)}, u32[]{:S(2)}, u32[]{:S(2)}) collective-permute-start(bf16[384,576]{0,1:T(8,128)(2,1)} %collective-permute-done), channel_id=1, source_target_pairs={{0,2},{1,3},{2,0},{3,1},{4,6},{5,7},{6,4},{7,5},{8,10},{9,11},{10,... | collective-permute-start | bytes 1327112 | tf_op jit(solution)/shard_map/ppermute | solution.py:19
  28.6 16.9 %collective-permute-start.6 = (bf16[384,576]{0,1:T(8,128)(2,1)S(1)}, bf16[384,576]{0,1:T(8,128)(2,1)S(1)}, u32[]{:S(2)}, u32[]{:S(2)}) collective-permute-start(bf16[384,576]{0,1:T(8,128)(2,1)S(1)} %collective-permute-done.5), channel_id=1, source_target_pairs={{2,0},{3,1},{6,4},{7,5},{10,8},{11,9},{14,12},{15,13},{18,16},{19,... | collective-permute-start | bytes 1327112 | tf_op jit(solution)/shard_map/ppermute | solution.py:19
  48.8 1.4 %copy-start.7 = (bf16[384,576]{0,1:T(8,128)(2,1)S(1)}, bf16[384,576]{0,1:T(8,128)(2,1)}, u32[]{:S(2)}) copy-start(bf16[384,576]{0,1:T(8,128)(2,1)} %param.6) | copy-start | bytes 1327108
  51.8 15.0 %collective-permute-start.3 = (bf16[384,576]{0,1:T(8,128)(2,1)S(1)}, bf16[384,576]{0,1:T(8,128)(2,1)S(1)}, u32[]{:S(2)}, u32[]{:S(2)}) collective-permute-start(bf16[384,576]{0,1:T(8,128)(2,1)S(1)} %broadcast_select_fusion.5), channel_id=1, source_target_pairs={{0,1},{1,0},{2,3},{3,2},{4,5},{5,4},{6,7},{7,6},{8,9},{9,8},{10,11... | collective-permute-start | bytes 1327112 | tf_op jit(solution)/shard_map/ppermute | solution.py:19
  52.2 10.3 %collective-permute-start.4 = (bf16[384,576]{0,1:T(8,128)(2,1)S(1)}, bf16[384,576]{0,1:T(8,128)(2,1)S(1)}, u32[]{:S(2)}, u32[]{:S(2)}) collective-permute-start(bf16[384,576]{0,1:T(8,128)(2,1)S(1)} %get-tuple-element.11), channel_id=1, source_target_pairs={{0,1},{1,0},{2,3},{3,2},{4,5},{5,4},{6,7},{7,6},{8,9},{9,8},{10,11... | collective-permute-start | bytes 1327112 | tf_op jit(solution)/shard_map/ppermute | solution.py:19
  52.3 6.3 %collective-permute-start.7 = (bf16[384,576]{0,1:T(8,128)(2,1)S(1)}, bf16[384,576]{0,1:T(8,128)(2,1)S(1)}, u32[]{:S(2)}, u32[]{:S(2)}) collective-permute-start(bf16[384,576]{0,1:T(8,128)(2,1)S(1)} %get-tuple-element.15), channel_id=1, source_target_pairs={{0,1},{1,0},{2,3},{3,2},{4,5},{5,4},{6,7},{7,6},{8,9},{9,8},{10,11... | collective-permute-start | bytes 1327112 | tf_op jit(solution)/shard_map/ppermute | solution.py:19
  52.7 2.8 %collective-permute-start.8 = (bf16[384,576]{0,1:T(8,128)(2,1)S(1)}, bf16[384,576]{0,1:T(8,128)(2,1)S(1)}, u32[]{:S(2)}, u32[]{:S(2)}) collective-permute-start(bf16[384,576]{0,1:T(8,128)(2,1)S(1)} %get-tuple-element.9), channel_id=1, source_target_pairs={{0,1},{1,0},{2,3},{3,2},{4,5},{5,4},{6,7},{7,6},{8,9},{9,8},{10,11... | collective-permute-start | bytes 1327112 | tf_op jit(solution)/shard_map/ppermute | solution.py:19

commit v5 on v4

--- a/solution.py
+++ b/solution.py
@@ -13,6 +13,7 @@
 DV = 128
 R = 512
 REACH = 7
+EARLY = (0, 2, 4)
 
 
 def moved(value, pairs):
@@ -41,12 +42,17 @@
     return moved(sent, [(s, s ^ 1) for s in range(count)])
 
 
-def attend_kernel(flag_ref, qn_ref, qr_ref, rel_ref, *rest):
-    blocks = REACH + 1
+def attend_kernel(distances, carry, flag_ref, qn_ref, qr_ref, rel_ref, *rest):
+    blocks = len(distances)
     rope_refs = rest[:blocks]
     key_refs = rest[blocks : 2 * blocks]
     value_refs = rest[2 * blocks : 3 * blocks]
-    out_ref, o_sc, m_sc, l_sc, bias_sc = rest[3 * blocks :]
+    rest = rest[3 * blocks :]
+    if carry:
+        num_in_ref, stat_in_ref = rest[:2]
+        rest = rest[2:]
+    outs = rest[: 1 if carry else 2]
+    o_sc, m_sc, l_sc, bias_sc = rest[len(outs) :]
     rows = value_refs[0].shape[0]
     score_scale = 1.0 / math.sqrt(DN + DR)
 
@@ -54,70 +60,92 @@
     def _():
         col = lax.broadcasted_iota(jnp.int32, (rows, rows), 1)
         rel = rel_ref[...]
-        for distance in range(REACH + 1):
+        for slot, distance in enumerate(distances):
             allowed = col >= rel + distance * rows
             if distance == 0:
                 allowed = allowed & (col <= lax.broadcasted_iota(jnp.int32, (rows, rows), 0))
-            bias_sc[distance] = jnp.where(allowed, jnp.float32(0.0), -jnp.inf)
-
-    for distance in range(REACH + 1):
-        rope_ref = rope_refs[distance]
-        key_ref = key_refs[distance]
-        value_ref = value_refs[distance]
-
-        @pl.when(flag_ref[distance] == 0)
+            bias_sc[slot] = jnp.where(allowed, jnp.float32(0.0), -jnp.inf)
+
+    for slot in range(blocks):
+        rope_ref = rope_refs[slot]
+        key_ref = key_refs[slot]
+        value_ref = value_refs[slot]
+
+        @pl.when(flag_ref[slot] == 0)
         def _():
-            o_sc[distance] = jnp.zeros((rows, DV), jnp.float32)
-            m_sc[distance] = jnp.full((rows, 1), -1e30, jnp.float32)
-            l_sc[distance] = jnp.zeros((rows, 1), jnp.float32)
-
-        @pl.when(flag_ref[distance] != 0)
+            o_sc[slot] = jnp.zeros((rows, DV), jnp.float32)
+            m_sc[slot] = jnp.full((rows, 1), -1e30, jnp.float32)
+            l_sc[slot] = jnp.zeros((rows, 1), jnp.float32)
+
+        @pl.when(flag_ref[slot] != 0)
         def _():
             scores = jnp.dot(qn_ref[0], key_ref[...], preferred_element_type=jnp.float32)
             scores = scores + jnp.dot(qr_ref[0], rope_ref[...], preferred_element_type=jnp.float32)
-            masked = scores * score_scale + bias_sc[distance]
+            masked = scores * score_scale + bias_sc[slot]
             block_max = jnp.maximum(jnp.max(masked, axis=1, keepdims=True), jnp.float32(-1e30))
             weights = jnp.exp(masked - block_max)
-            l_sc[distance] = jnp.sum(weights, axis=1, keepdims=True)
-            m_sc[distance] = block_max
-            o_sc[distance] = jnp.dot(
-                weights.astype(jnp.bfloat16), value_ref[...], preferred_element_type=jnp.float32
-            )
+            l_sc[slot] = jnp.sum(weights, axis=1, keepdims=True)
+            m_sc[slot] = block_max
+            o_sc[slot] = jnp.dot(weights.astype(jnp.bfloat16), value_ref[...], preferred_element_type=jnp.float32)
 
     top_max = m_sc[0]
-    for distance in range(1, REACH + 1):
-        top_max = jnp.maximum(top_max, m_sc[distance])
-    numerator = jnp.zeros((rows, DV), jnp.float32)
-    denominator = jnp.zeros((rows, 1), jnp.float32)
-    for distance in range(REACH + 1):
-        factor = jnp.exp(m_sc[distance] - top_max)
-        numerator = numerator + factor * o_sc[distance]
-        denominator = denominator + factor * l_sc[distance]
-    out_ref[...] = (numerator / denominator).astype(out_ref.dtype)
-
-
-def attend(flags, query_nope, query_rope, rel_start, rope_blocks, key_blocks, value_blocks):
+    for slot in range(1, blocks):
+        top_max = jnp.maximum(top_max, m_sc[slot])
+    if carry:
+        stat_in = stat_in_ref[...]
+        carried_max = stat_in[:, 0:1]
+        top_max = jnp.maximum(top_max, carried_max)
+        carried = jnp.exp(carried_max - top_max)
+        numerator = carried * num_in_ref[...]
+        denominator = carried * stat_in[:, DV // 2 : DV // 2 + 1]
+    else:
+        numerator = jnp.zeros((rows, DV), jnp.float32)
+        denominator = jnp.zeros((rows, 1), jnp.float32)
+    for slot in range(blocks):
+        factor = jnp.exp(m_sc[slot] - top_max)
+        numerator = numerator + factor * o_sc[slot]
+        denominator = denominator + factor * l_sc[slot]
+    if carry:
+        outs[0][...] = (numerator / denominator).astype(outs[0].dtype)
+    else:
+        lane = lax.broadcasted_iota(jnp.int32, (rows, DV), 1)
+        outs[0][...] = numerator
+        outs[1][...] = jnp.where(lane < DV // 2, top_max, denominator)
+
+
+def attend(distances, flags, query_nope, query_rope, rel_start, rope_blocks, key_blocks, value_blocks, state=None):
     head_count, rows, _ = query_nope.shape
-    blocks = len(rope_blocks)
+    blocks = len(distances)
+    carry = state is not None
     flops = head_count * blocks * rows * 2 * rows * (DN + DR + DV)
     rope_spec = pl.BlockSpec((DR, rows), lambda h, f: (0, 0))
     key_spec = pl.BlockSpec((DN, rows), lambda h, f: (h, 0))
-    value_spec = pl.BlockSpec((rows, DV), lambda h, f: (0, h))
+    head_spec = pl.BlockSpec((rows, DV), lambda h, f: (0, h))
+    in_specs = [
+        pl.BlockSpec((1, rows, DN), lambda h, f: (h, 0, 0)),
+        pl.BlockSpec((1, rows, DR), lambda h, f: (h, 0, 0)),
+        pl.BlockSpec((rows, 1), lambda h, f: (0, 0)),
+    ] + [rope_spec] * blocks + [key_spec] * blocks + [head_spec] * blocks
+    operands = [flags, query_nope, query_rope, rel_start, *rope_blocks, *key_blocks, *value_blocks]
+    if carry:
+        in_specs += [head_spec, head_spec]
+        operands += list(state)
+        out_shape = jax.ShapeDtypeStruct((rows, head_count * DV), jnp.bfloat16)
+        out_specs = head_spec
+    else:
+        out_shape = (
+            jax.ShapeDtypeStruct((rows, head_count * DV), jnp.float32),
+            jax.ShapeDtypeStruct((rows, head_count * DV), jnp.float32),
+        )
+        out_specs = [head_spec, head_spec]
     return pl.pallas_call(
-        attend_kernel,
-        out_shape=jax.ShapeDtypeStruct((rows, head_count * DV), jnp.bfloat16),
+        functools.partial(attend_kernel, tuple(distances), carry),
+        out_shape=out_shape,
         grid_spec=pltpu.PrefetchScalarGridSpec(
             num_scalar_prefetch=1,
             grid=(head_count,),
-            in_specs=[
-                pl.BlockSpec((1, rows, DN), lambda h, f: (h, 0, 0)),
-                pl.BlockSpec((1, rows, DR), lambda h, f: (h, 0, 0)),
-                pl.BlockSpec((rows, 1), lambda h, f: (0, 0)),
-            ]
-            + [rope_spec] * blocks
-            + [key_spec] * blocks
-            + [value_spec] * blocks,
-            out_specs=pl.BlockSpec((rows, DV), lambda h, f: (0, h)),
+            in_specs=in_specs,
+            out_specs=out_specs,
             scratch_shapes=[
                 pltpu.VMEM((blocks, rows, DV), jnp.float32),
                 pltpu.VMEM((blocks, rows, 1), jnp.float32),
@@ -127,9 +155,9 @@
         ),
         compiler_params=pltpu.CompilerParams(dimension_semantics=("arbitrary",)),
         cost_estimate=pl.CostEstimate(
-            flops=flops, transcendentals=head_count * blocks * rows * rows, bytes_accessed=16 * 1024 * 1024
+            flops=flops, transcendentals=head_count * blocks * rows * rows, bytes_accessed=2 * blocks * 1024 * 1024
         ),
-    )(flags, query_nope, query_rope, rel_start, *rope_blocks, *key_blocks, *value_blocks)
+    )(*operands)
 
 
 def local(queries, latent_rope, doc_start, w_kv_up, w_out):
@@ -163,7 +191,22 @@
         for block in latent_blocks
     ]
     rope_blocks = [block[:, R:].T for block in latent_blocks]
-    attended = attend(flags, query_nope, query_rope, rel_start, rope_blocks, key_blocks, value_blocks)
+
+    def group(chosen, state=None):
+        return attend(
+            chosen,
+            flags[jnp.array(chosen)],
+            query_nope,
+            query_rope,
+            rel_start,
+            [rope_blocks[d] for d in chosen],
+            [key_blocks[d] for d in chosen],
+            [value_blocks[d] for d in chosen],
+            state,
+        )
+
+    early = group(EARLY)
+    attended = group(tuple(d for d in range(REACH + 1) if d not in EARLY), early)
     return jnp.dot(attended, w_out, preferred_element_type=jnp.float32).astype(jnp.bfloat16)
 
 

time: 118 us -> 136 us (1.15)
  matrix products: 32.4 us -> 39.8 us
  local copies, waits for them, and re-layouts: 13.5 us -> 19.8 us
  Pallas kernels: 41.3 us -> 46.5 us
  starting transfers between devices: 12.8 us -> 11.1 us
    pallas_call x1 -> x2, Pallas kernels: 41.3 us -> 46.5 us  [attend(): pl.pallas_call(functools.partial(attend_kernel, tuple(distances), carry),...]
    dot_general x8, matrix products: 13.8 us -> 18.1 us  [local(): jnp.einsum('jr,rc->cj', block[:, :R], w_key, preferred_element_type=jnp.f...]
    dot_general x8, matrix products: 13.3 us -> 16.3 us  [local(): jnp.dot(block[:, :R], w_value, preferred_element_type=jnp.float32)]
    transpose x7 -> x8, local copies, waits for them, and re-layouts: 5.17 us -> 8.14 us  [local(): rope_blocks = [block[:, R:].T for block in latent_blocks]]
    gather x0 -> x2, local copies, waits for them, and re-layouts: none -> 2.39 us  [group(): flags[jnp.array(chosen)]]
    select_n x3, other arithmetic: 1.55 us -> 3.2 us  [odd_distance_block(): sent = jnp.where(upper_core, farther, nearer)]
    ppermute x9, starting transfers between devices: 12.8 us -> 11.1 us  [moved(): return lax.ppermute(value, 'srv', pairs)]
    unnamed x20 -> x10, local copies, waits for them, and re-layouts: 4.58 us -> 4.58 us
  transfers between devices with their start and end apart: 9 -> 9, of which waited for: 5 -> 2; matrix products, arithmetic and copies ran while one was open for 31% -> 30% of each run, Pallas kernels for 0% -> 15%
where the time goes in v5:
time: 136 us; the launch traced here: 134 us
  Pallas kernels  46.5 us (34%)
  matrix products  39.8 us (29%)
  local copies, waits for them, and re-layouts  19.8 us (15%)
  waiting for transfers between devices  12.4 us (9%)
  starting transfers between devices  11.1 us (8%)
  other arithmetic  4.43 us (3%)
    pallas_call x2, Pallas kernels, attend(): pl.pallas_call(functools.partial(attend_kernel, tuple(distances), carry),...  46.5 us
    dot_general x8, matrix products, local(): jnp.einsum('jr,rc->cj', block[:, :R], w_key, preferred_element_type=jnp.f...  18.1 us
    dot_general x8, matrix products, local(): jnp.dot(block[:, :R], w_value, preferred_element_type=jnp.float32)  16.3 us
    ppermute x9, waiting for transfers between devices, moved(): return lax.ppermute(value, 'srv', pairs)  12.4 us
    ppermute x9, starting transfers between devices, moved(): return lax.ppermute(value, 'srv', pairs)  11.1 us
    transpose x8, local copies, waits for them, and re-layouts, local(): rope_blocks = [block[:, R:].T for block in latent_blocks]  8.14 us
    dot_general x1, matrix products, local(): jnp.dot(attended, w_out, preferred_element_type=jnp.float32)  5.37 us
    unnamed x10, local copies, waits for them, and re-layouts  4.58 us
  transfers between devices with their start and end apart: 9, of which 2 were waited for; matrix products, arithmetic and copies ran while one was open for 30% of the time, Pallas kernels for 15%

profile of v5, /device:TPU:10, one launch (start us, length us, event | category | flops | bytes accessed | tf_op | source)
XLA Modules:
  0.0 134.2 jit_solution(16937950374718340129)
XLA Ops:
  0.0 3.5 %collective-permute-start = (bf16[384,576]{0,1:T(8,128)(2,1)}, bf16[384,576]{0,1:T(8,128)(2,1)}, u32[]{:S(2)}, u32[]{:S(2)}) collective-permute-start(bf16[384,576]{0,1:T(8,128)(2,1)} %param.8), channel_id=1, source_target_pairs={{0,4},{1,5},{2,6},{3,7},{4,8},{5,9},{6,10},{7,11},{8,12},{9,13},{1... | collective-permute-start | bytes 1327112 | tf_op jit(solution)/shard_map/ppermute | solution.py:20
  3.5 1.3 collective-permute-start.2
  4.8 1.7 %copy.16 = bf16[384,1536]{0,1:T(8,128)(2,1)S(1)} copy(bf16[384,1536]{1,0:T(8,128)(2,1)} %param.7) | data formatting | bytes 2359296 | tf_op args[0]
  6.5 0.7 copy.17
  7.2 1.0 slice.92.qn_ref
  8.3 1.0 slice.93.qr_ref
  9.3 2.9 %copy.18 = bf16[512,2048]{0,1:T(8,128)(2,1)S(1)} copy(bf16[512,2048]{1,0:T(8,128)(2,1)} %param.10) | data formatting | bytes 4194304 | tf_op args[3]
  12.2 0.0 copy-start.2
  12.2 0.0 copy-start.3
  12.2 1.2 fusion.18
  13.4 0.0 copy-done.2
  13.4 0.6 broadcast_subtract_fusion
  14.0 0.6 compare_convert_fusion
  14.6 0.8 reshape.29.rel_ref
  15.4 0.0 copy-done.3
  15.4 1.2 gather_fusion.1
  16.6 1.2 gather_fusion
  17.8 2.9 %convolution_convert_fusion.6.rest_3_ = bf16[1024,384]{1,0:T(8,128)(2,1)} fusion(bf16[512,1024]{0,1:T(8,128)(2,1)} %bitcast.55, bf16[384,576]{0,1:T(8,128)(2,1)} %param.8), kind=kOutput, calls=%fused_computation.8 | convolution fusion | flops 403046400 | bytes 2228224 | tf_op jit(solution)/shard_map/jr,rc->cj/dot_general | solution.py:186
  20.7 0.0 copy-done.1
  20.7 1.5 %fusion.rest_6_ = bf16[384,1024]{1,0:T(8,128)(2,1)} fusion(bf16[512,1024]{0,1:T(8,128)(2,1)S(1)} %bitcast.47, bf16[384,576]{0,1:T(8,128)(2,1)S(1)} %copy-done.1), kind=kOutput, calls=%fused_computation.19 | convolution fusion | flops 403046400 | bytes 2228224 | tf_op jit(solution)/shard_map/dot_general | solution.py:190
  22.2 0.0 collective-permute-done
  22.2 3.5 %collective-permute-start.5 = (bf16[384,576]{0,1:T(8,128)(2,1)}, bf16[384,576]{0,1:T(8,128)(2,1)S(1)}, u32[]{:S(2)}, u32[]{:S(2)}) collective-permute-start(bf16[384,576]{0,1:T(8,128)(2,1)} %collective-permute-done), channel_id=1, source_target_pairs={{1,5},{2,6},{3,7},{5,9},{6,10},{7,11},{9,13},{10,14},{11,15},{17,2... | collective-permute-start | bytes 1327112 | tf_op jit(solution)/shard_map/ppermute | solution.py:20
  25.7 0.6 slice_bitcast_fusion.7.rest_0_
  26.3 0.6 collective-permute-start.1
  26.9 2.6 %convolution_convert_fusion.4.rest_5_ = bf16[1024,384]{1,0:T(8,128)(2,1)} fusion(bf16[512,1024]{0,1:T(8,128)(2,1)S(1)} %bitcast.56, bf16[384,576]{0,1:T(8,128)(2,1)} %collective-permute-done), kind=kOutput, calls=%fused_computation.6 | convolution fusion | flops 403046400 | bytes 2228224 | tf_op jit(solution)/shard_map/jr,rc->cj/dot_general | solution.py:186
  29.5 6.4 %collective-permute-done.5 = bf16[384,576]{0,1:T(8,128)(2,1)S(1)} collective-permute-done((bf16[384,576]{0,1:T(8,128)(2,1)}, bf16[384,576]{0,1:T(8,128)(2,1)S(1)}, u32[]{:S(2)}, u32[]{:S(2)}) %collective-permute-start.5) | collective-permute-done | bytes 442400 | tf_op jit(solution)/shard_map/ppermute | solution.py:20
  35.9 1.3 collective-permute-start.6
  37.2 2.5 %fusion.1.rest_8_ = bf16[384,1024]{1,0:T(8,128)(2,1)} fusion(bf16[512,1024]{0,1:T(8,128)(2,1)S(1)} %bitcast.48, bf16[384,576]{0,1:T(8,128)(2,1)} %collective-permute-done), kind=kOutput, calls=%fused_computation.20 | convolution fusion | flops 403046400 | bytes 2228224 | tf_op jit(solution)/shard_map/dot_general | solution.py:190
  39.8 1.4 %slice_bitcast_fusion.rest_2_ = bf16[64,384]{1,0:T(8,128)(2,1)} fusion(bf16[384,576]{0,1:T(8,128)(2,1)} %collective-permute-done), kind=kLoop, calls=%fused_computation.43 | loop fusion | bytes 98304 | tf_op jit(solution)/shard_map/transpose | solution.py:193
  41.2 0.0 collective-permute-done.1
  41.2 6.0 %collective-permute-done.6 = bf16[384,576]{0,1:T(8,128)(2,1)S(1)} collective-permute-done((bf16[384,576]{0,1:T(8,128)(2,1)S(1)}, bf16[384,576]{0,1:T(8,128)(2,1)S(1)}, u32[]{:S(2)}, u32[]{:S(2)}) %collective-permute-start.6) | collective-permute-done | bytes 442400 | tf_op jit(solution)/shard_map/ppermute | solution.py:20
  47.1 0.9 broadcast_select_fusion.2
  48.0 0.0 collective-permute-done.2
  48.0 2.3 %broadcast_select_fusion.4 = (bf16[384,576]{0,1:T(8,128)(2,1)}, bf16[384,576]{0,1:T(8,128)(2,1)S(1)}, bf16[384,576]{0,1:T(8,128)(2,1)}) fusion(bf16[384,576]{0,1:T(8,128)(2,1)} %collective-permute-done, pred[]{:T(512)S(6)} %eq.12, bf16[384,576]{0,1:T(8,128)(2,1)S(1)} %collective-permute-done.1, bf16[384,576]{0,1:T(8,128)(2,1)} %collective-permute-done.2, ...), kind=kLoop, calls=%fused_computation.25 | loop fusion | flops 663552 | bytes 3096578 | tf_op jit(solution)/shard_map/jit(_where)/select_n | solution.py:41
  50.3 1.6 %convolution_convert_fusion.2.rest_7_ = bf16[384,1024]{1,0:T(8,128)(2,1)} fusion(bf16[512,1024]{0,1:T(8,128)(2,1)S(1)} %bitcast.49, bf16[384,576]{0,1:T(8,128)(2,1)S(1)} %get-tuple-element.16), kind=kOutput, calls=%fused_computation.4 | convolution fusion | flops 403046400 | bytes 2228224 | tf_op jit(solution)/shard_map/dot_general | solution.py:190
  51.9 1.6 %convolution_convert_fusion.5.rest_4_ = bf16[1024,384]{1,0:T(8,128)(2,1)} fusion(bf16[512,1024]{0,1:T(8,128)(2,1)S(1)} %bitcast.57, bf16[384,576]{0,1:T(8,128)(2,1)S(1)} %get-tuple-element.16), kind=kOutput, calls=%fused_computation.7 | convolution fusion | flops 403046400 | bytes 2228224 | tf_op jit(solution)/shard_map/jr,rc->cj/dot_general | solution.py:186
  53.5 0.6 slice_bitcast_fusion.1.rest_1_
  54.1 0.1 broadcast_select_fusion.5
  54.1 1.6 %convolution_convert_fusion.13.rest_8_ = bf16[1024,384]{1,0:T(8,128)(2,1)} fusion(bf16[512,1024]{0,1:T(8,128)(2,1)S(1)} %bitcast.58, bf16[384,576]{0,1:T(8,128)(2,1)S(1)} %get-tuple-element.14), kind=kOutput, calls=%fused_computation.15 | convolution fusion | flops 403046400 | bytes 2228224 | tf_op jit(solution)/shard_map/jr,rc->cj/dot_general | solution.py:186
  55.8 0.6 slice_bitcast_fusion.3.rest_3_
  56.4 0.0 collective-permute-start.3
  56.4 0.5 collective-permute-start.4
  56.9 0.0 collective-permute-start.7
  56.9 0.5 collective-permute-start.8
  57.4 19.7 %shard_map.73 = (f32[384,1024]{1,0:T(8,128)}, f32[384,1024]{1,0:T(8,128)}) custom-call(s32[3]{0:T(128)} %gather_fusion.1, bf16[8,384,128]{2,1,0:T(8,128)(2,1)} %slice.92.qn_ref, bf16[8,384,64]{2,1,0:T(8,128)(2,1)} %slice.93.qr_ref, s32[384,1]{1,0:T(8,128)} %reshape.29.rel_ref, bf16[64,384]{1,0:T(8,128)(2,1)} %slice_bitcast_fusion.7.rest_0_, ...), custom_call_target="tpu_custom_call" | custom-call | flops 2264924160 | bytes 6291456 | tf_op jit(solution)/shard_map/pallas_call | solution.py:141
  77.1 1.5 %convolution_convert_fusion.8.rest_13_ = bf16[384,1024]{1,0:T(8,128)(2,1)} fusion(bf16[512,1024]{0,1:T(8,128)(2,1)S(1)} %bitcast.50, bf16[384,576]{0,1:T(8,128)(2,1)S(1)} %get-tuple-element.14), kind=kOutput, calls=%fused_computation.10 | convolution fusion | flops 403046400 | bytes 2228224 | tf_op jit(solution)/shard_map/dot_general | solution.py:190
  78.6 0.0 collective-permute-done.4
  78.6 2.5 %convolution_convert_fusion.10.rest_11_ = bf16[384,1024]{1,0:T(8,128)(2,1)} fusion(bf16[512,1024]{0,1:T(8,128)(2,1)S(1)} %bitcast.51, bf16[384,576]{0,1:T(8,128)(2,1)} %collective-permute-done.4), kind=kOutput, calls=%fused_computation.12 | convolution fusion | flops 403046400 | bytes 2228224 | tf_op jit(solution)/shard_map/dot_general | solution.py:190
  81.1 2.6 %convolution_convert_fusion.15.rest_6_ = bf16[1024,384]{1,0:T(8,128)(2,1)} fusion(bf16[512,1024]{0,1:T(8,128)(2,1)S(1)} %bitcast.59, bf16[384,576]{0,1:T(8,128)(2,1)} %collective-permute-done.4), kind=kOutput, calls=%fused_computation.17 | convolution fusion | flops 403046400 | bytes 2228224 | tf_op jit(solution)/shard_map/jr,rc->cj/dot_general | solution.py:186
  83.7 0.0 collective-permute-done.7
  83.7 2.6 %convolution_convert_fusion.14.rest_7_ = bf16[1024,384]{1,0:T(8,128)(2,1)} fusion(bf16[512,1024]{0,1:T(8,128)(2,1)S(1)} %bitcast.60, bf16[384,576]{0,1:T(8,128)(2,1)} %collective-permute-done.7), kind=kOutput, calls=%fused_computation.16 | convolution fusion | flops 403046400 | bytes 2228224 | tf_op jit(solution)/shard_map/jr,rc->cj/dot_general | solution.py:186
  86.3 2.6 %convolution_convert_fusion.9.rest_12_ = bf16[384,1024]{1,0:T(8,128)(2,1)} fusion(bf16[512,1024]{0,1:T(8,128)(2,1)S(1)} %bitcast.52, bf16[384,576]{0,1:T(8,128)(2,1)} %collective-permute-done.7), kind=kOutput, calls=%fused_computation.11 | convolution fusion | flops 403046400 | bytes 2228224 | tf_op jit(solution)/shard_map/dot_general | solution.py:190
  88.8 0.0 collective-permute-done.3
  88.8 1.6 %convolution_convert_fusion.11.rest_10_ = bf16[384,1024]{1,0:T(8,128)(2,1)} fusion(bf16[512,1024]{0,1:T(8,128)(2,1)S(1)} %bitcast.53, bf16[384,576]{0,1:T(8,128)(2,1)S(1)} %collective-permute-done.3), kind=kOutput, calls=%fused_computation.13 | convolution fusion | flops 403046400 | bytes 2228224 | tf_op jit(solution)/shard_map/dot_general | solution.py:190
  90.4 1.6 %convolution_convert_fusion.16.rest_5_ = bf16[1024,384]{1,0:T(8,128)(2,1)} fusion(bf16[512,1024]{0,1:T(8,128)(2,1)S(1)} %bitcast.61, bf16[384,576]{0,1:T(8,128)(2,1)S(1)} %collective-permute-done.3), kind=kOutput, calls=%fused_computation.18 | convolution fusion | flops 403046400 | bytes 2228224 | tf_op jit(solution)/shard_map/jr,rc->cj/dot_general | solution.py:186
  92.0 0.0 collective-permute-done.8
  92.0 2.6 %convolution_convert_fusion.12.rest_9_ = bf16[1024,384]{1,0:T(8,128)(2,1)} fusion(bf16[512,1024]{0,1:T(8,128)(2,1)S(1)} %bitcast.62, bf16[384,576]{0,1:T(8,128)(2,1)} %collective-permute-done.8), kind=kOutput, calls=%fused_computation.14 | convolution fusion | flops 403046400 | bytes 2228224 | tf_op jit(solution)/shard_map/jr,rc->cj/dot_general | solution.py:186
  94.6 2.5 %convolution_convert_fusion.7.rest_14_ = bf16[384,1024]{1,0:T(8,128)(2,1)} fusion(bf16[512,1024]{0,1:T(8,128)(2,1)S(1)} %bitcast.54, bf16[384,576]{0,1:T(8,128)(2,1)} %collective-permute-done.8), kind=kOutput, calls=%fused_computation.9 | convolution fusion | flops 403046400 | bytes 2228224 | tf_op jit(solution)/shard_map/dot_general | solution.py:190
  97.1 0.6 slice_bitcast_fusion.6.rest_0_
  97.8 1.4 %slice_bitcast_fusion.4.rest_2_ = bf16[64,384]{1,0:T(8,128)(2,1)} fusion(bf16[384,576]{0,1:T(8,128)(2,1)} %collective-permute-done.7), kind=kLoop, calls=%fused_computation.47 | loop fusion | bytes 98304 | tf_op jit(solution)/shard_map/transpose | solution.py:193
  99.2 1.4 %slice_bitcast_fusion.5.rest_1_ = bf16[64,384]{1,0:T(8,128)(2,1)} fusion(bf16[384,576]{0,1:T(8,128)(2,1)} %collective-permute-done.4), kind=kLoop, calls=%fused_computation.48 | loop fusion | bytes 98304 | tf_op jit(solution)/shard_map/transpose | solution.py:193
  100.6 1.4 %slice_bitcast_fusion.2.rest_4_ = bf16[64,384]{1,0:T(8,128)(2,1)} fusion(bf16[384,576]{0,1:T(8,128)(2,1)} %collective-permute-done.8), kind=kLoop, calls=%fused_computation.45 | loop fusion | bytes 98304 | tf_op jit(solution)/shard_map/transpose | solution.py:193
  102.0 26.9 %shard_map.74 = bf16[384,1024]{1,0:T(8,128)(2,1)} custom-call(s32[5]{0:T(128)} %gather_fusion, bf16[8,384,128]{2,1,0:T(8,128)(2,1)} %slice.92.qn_ref, bf16[8,384,64]{2,1,0:T(8,128)(2,1)} %slice.93.qr_ref, s32[384,1]{1,0:T(8,128)} %reshape.29.rel_ref, bf16[64,384]{1,0:T(8,128)(2,1)} %slice_bitcast_fusion.6.rest_0_, ...), custom_call_target="tpu_custom_call" | custom-call | flops 3774873600 | bytes 10485760 | tf_op jit(solution)/shard_map/pallas_call | solution.py:141
  128.9 5.4 %convolution_convert_fusion = bf16[384,2048]{1,0:T(8,128)(2,1)} fusion(bf16[384,1024]{1,0:T(8,128)(2,1)} %shard_map.74, bf16[1024,2048]{1,0:T(8,128)(2,1)} %param.11), kind=kOutput, calls=%fused_computation.2 | convolution fusion | flops 1611399168 | bytes 6553600 | tf_op jit(solution)/shard_map/dot_general | solution.py:210
  (6 shorter events, 0.0 us)
Async XLA Ops:
  0.0 22.2 %collective-permute-start = (bf16[384,576]{0,1:T(8,128)(2,1)}, bf16[384,576]{0,1:T(8,128)(2,1)}, u32[]{:S(2)}, u32[]{:S(2)}) collective-permute-start(bf16[384,576]{0,1:T(8,128)(2,1)} %param.8), channel_id=1, source_target_pairs={{0,4},{1,5},{2,6},{3,7},{4,8},{5,9},{6,10},{7,11},{8,12},{9,13},{1... | collective-permute-start | bytes 1327112 | tf_op jit(solution)/shard_map/ppermute | solution.py:20
  3.5 44.5 %collective-permute-start.2 = (bf16[384,576]{0,1:T(8,128)(2,1)}, bf16[384,576]{0,1:T(8,128)(2,1)}, u32[]{:S(2)}, u32[]{:S(2)}) collective-permute-start(bf16[384,576]{0,1:T(8,128)(2,1)} %param.8), channel_id=1, source_target_pairs={{0,2},{1,3},{4,6},{5,7},{8,10},{9,11},{12,14},{13,15},{16,18},{17,... | collective-permute-start | bytes 1327112 | tf_op jit(solution)/shard_map/ppermute | solution.py:20
  12.2 1.2 copy-start.2
  12.2 3.2 %copy-start.3 = (s32[5]{0:T(128)S(1)}, s32[5]{0:T(128)}, u32[]{:S(2)}) copy-start(s32[5]{0:T(128)} %constant.59) | copy-start | bytes 64
  16.6 4.1 %copy-start.1 = (bf16[384,576]{0,1:T(8,128)(2,1)S(1)}, bf16[384,576]{0,1:T(8,128)(2,1)}, u32[]{:S(2)}) copy-start(bf16[384,576]{0,1:T(8,128)(2,1)} %param.8) | copy-start | bytes 1327108
  20.7 6.2 %copy-start = (bf16[512,8,1,128]{0,3,2,1:T(8,128)(2,1)S(1)}, bf16[512,8,1,128]{0,3,2,1:T(8,128)(2,1)}, u32[]{:S(2)}) copy-start(bf16[512,8,1,128]{0,3,2,1:T(8,128)(2,1)} %get-tuple-element.18) | copy-start | bytes 3145732
  22.2 13.7 %collective-permute-start.5 = (bf16[384,576]{0,1:T(8,128)(2,1)}, bf16[384,576]{0,1:T(8,128)(2,1)S(1)}, u32[]{:S(2)}, u32[]{:S(2)}) collective-permute-start(bf16[384,576]{0,1:T(8,128)(2,1)} %collective-permute-done), channel_id=1, source_target_pairs={{1,5},{2,6},{3,7},{5,9},{6,10},{7,11},{9,13},{10,14},{11,15},{17,2... | collective-permute-start | bytes 1327112 | tf_op jit(solution)/shard_map/ppermute | solution.py:20
  26.3 14.9 %collective-permute-start.1 = (bf16[384,576]{0,1:T(8,128)(2,1)}, bf16[384,576]{0,1:T(8,128)(2,1)S(1)}, u32[]{:S(2)}, u32[]{:S(2)}) collective-permute-start(bf16[384,576]{0,1:T(8,128)(2,1)} %collective-permute-done), channel_id=1, source_target_pairs={{0,2},{1,3},{2,0},{3,1},{4,6},{5,7},{6,4},{7,5},{8,10},{9,11},{10,... | collective-permute-start | bytes 1327112 | tf_op jit(solution)/shard_map/ppermute | solution.py:20
  35.9 11.2 %collective-permute-start.6 = (bf16[384,576]{0,1:T(8,128)(2,1)S(1)}, bf16[384,576]{0,1:T(8,128)(2,1)S(1)}, u32[]{:S(2)}, u32[]{:S(2)}) collective-permute-start(bf16[384,576]{0,1:T(8,128)(2,1)S(1)} %collective-permute-done.5), channel_id=1, source_target_pairs={{2,0},{3,1},{6,4},{7,5},{10,8},{11,9},{14,12},{15,13},{18,16},{19,... | collective-permute-start | bytes 1327112 | tf_op jit(solution)/shard_map/ppermute | solution.py:20
  56.4 32.5 %collective-permute-start.3 = (bf16[384,576]{0,1:T(8,128)(2,1)S(1)}, bf16[384,576]{0,1:T(8,128)(2,1)S(1)}, u32[]{:S(2)}, u32[]{:S(2)}) collective-permute-start(bf16[384,576]{0,1:T(8,128)(2,1)S(1)} %broadcast_select_fusion.5), channel_id=1, source_target_pairs={{0,1},{1,0},{2,3},{3,2},{4,5},{5,4},{6,7},{7,6},{8,9},{9,8},{10,11... | collective-permute-start | bytes 1327112 | tf_op jit(solution)/shard_map/ppermute | solution.py:20
  56.4 22.2 %collective-permute-start.4 = (bf16[384,576]{0,1:T(8,128)(2,1)}, bf16[384,576]{0,1:T(8,128)(2,1)}, u32[]{:S(2)}, u32[]{:S(2)}) collective-permute-start(bf16[384,576]{0,1:T(8,128)(2,1)} %get-tuple-element.15), channel_id=1, source_target_pairs={{0,1},{1,0},{2,3},{3,2},{4,5},{5,4},{6,7},{7,6},{8,9},{9,8},{10,11... | collective-permute-start | bytes 1327112 | tf_op jit(solution)/shard_map/ppermute | solution.py:20
  56.9 26.8 %collective-permute-start.7 = (bf16[384,576]{0,1:T(8,128)(2,1)}, bf16[384,576]{0,1:T(8,128)(2,1)}, u32[]{:S(2)}, u32[]{:S(2)}) collective-permute-start(bf16[384,576]{0,1:T(8,128)(2,1)} %get-tuple-element.19), channel_id=1, source_target_pairs={{0,1},{1,0},{2,3},{3,2},{4,5},{5,4},{6,7},{7,6},{8,9},{9,8},{10,11... | collective-permute-start | bytes 1327112 | tf_op jit(solution)/shard_map/ppermute | solution.py:20
  56.9 35.2 %collective-permute-start.8 = (bf16[384,576]{0,1:T(8,128)(2,1)}, bf16[384,576]{0,1:T(8,128)(2,1)}, u32[]{:S(2)}, u32[]{:S(2)}) collective-permute-start(bf16[384,576]{0,1:T(8,128)(2,1)} %get-tuple-element.13), channel_id=1, source_target_pairs={{0,1},{1,0},{2,3},{3,2},{4,5},{5,4},{6,7},{7,6},{8,9},{9,8},{10,11... | collective-permute-start | bytes 1327112 | tf_op jit(solution)/shard_map/ppermute | solution.py:20
